TPU v7x, 256 devices: a whole 4x4x8 slice. The times are simulated.
256 devices in a mesh: gx: 8 (over x_lo, y), gy: 32 (over x_hi, z, core).
Axes of the slice: x: 4 (x_hi: 2, x_lo: 2; x = x_hi * 2 + x_lo), y: 4, z: 8, core: 2. Of those that a mesh axis runs over, the one named last changes fastest.
Arguments:
- source: bfloat16 [288, 8, 32, 1024], P(None, 'gx', 'gy'), may hold values from -6 to 6
- slope: float32 [2, 144], replicated, may hold values from -6 to 6
- quad: bfloat16 [4, 4, 2, 20736], replicated, may hold values from -1 to 1, as said below
- pair: bfloat16 [2, 2, 2, 20736], replicated, may hold values from -1 to 1, as said below
Outputs:
- image: bfloat16 [288, 8, 32, 1024], P(None, 'gx', 'gy')
Inputs may be any that keep to these rules, and one draw needn't show every extreme that they name: `quad`: translation coefficients. `pair`: translation coefficients.
All inputs are finite; a program needn't handle non-finite values.
Results may differ from a plain program's by a relative error of at most 0.02.
Values may be sent and summed in bfloat16 or wider, within the bound.
No kernel may reach another device: no remote copies, remote signals or barrier semaphores. Data moves between devices by JAX's collectives and lax.ppermute only.
A program may use at most 64 MiB of HBM per device.

v0:
```python
import functools

import jax
import jax.numpy as jnp
from jax import lax
from jax.experimental import pallas as pl
from jax.experimental.pallas import tpu as pltpu
from jax.sharding import PartitionSpec as P

P_SIZE = 144
SIDE = 32
LANE = 256
WIDE = 384
F = 2 * P_SIZE


def padded(x):
    x = x.reshape(x.shape[:-2] + (F,))
    pad = [(0, 0)] * (x.ndim - 1) + [(0, WIDE - F)]
    return jnp.pad(x, pad)


def build_weights(wt_ref, m_ref):
    count = wt_ref.shape[0]
    zeros = jnp.zeros((P_SIZE, 128), jnp.float32)

    def ext(v):
        return jnp.concatenate([v, zeros], 1)

    for t in range(count):
        wt_ref[t, F:WIDE, :] = jnp.zeros((WIDE - F, wt_ref.shape[2]), wt_ref.dtype)
        for c in range(count):
            real = ext(m_ref[t, c, 0].astype(jnp.float32))
            imag = ext(m_ref[t, c, 1].astype(jnp.float32))
            top = real + pltpu.roll(-imag, P_SIZE, 1)
            bottom = imag + pltpu.roll(real, P_SIZE, 1)
            base = c * WIDE
            wt_ref[t, 0:P_SIZE, base:base + WIDE] = top.astype(wt_ref.dtype)
            wt_ref[t, P_SIZE:F, base:base + WIDE] = bottom.astype(wt_ref.dtype)


def class_pieces(fixed, rows):
    low = min(fixed)
    base = sum(v << p for p, v in fixed.items())
    free = [p for p in range(rows.bit_length() - 1) if p not in fixed]
    if (1 << low) >= 8:
        outer = [p for p in free if p > low]
        starts = []
        for k in range(1 << len(outer)):
            starts.append(base + sum(((k >> i) & 1) << p for i, p in enumerate(outer)))
        return [pl.ds(st, 1 << low) for st in starts]
    above = [p for p in fixed if p > low]
    top = min(above) if above else rows.bit_length() - 1
    inner = [p for p in free if low < p < top]
    outer = [p for p in free if p < low or p > top]
    slices = []
    for k in range(1 << len(outer)):
        st = base + sum(((k >> i) & 1) << p for i, p in enumerate(outer))
        slices.append(pl.ds(st, 1 << len(inner), stride=1 << (low + 1)))
    return slices


def load_class(ref, fixed):
    chunks, rows = ref.shape[:2]
    pieces = []
    for s in class_pieces(fixed, rows):
        parts = [ref[q, s, :] for q in range(chunks)]
        pieces.append(jnp.concatenate(parts, 1))
    return pieces[0] if len(pieces) == 1 else jnp.concatenate(pieces, 0)


def store_class(ref, fixed, value):
    chunks, rows = ref.shape[:2]
    at = 0
    for s in class_pieces(fixed, rows):
        size = s.size
        for q in range(chunks):
            ref[q, s, :] = value[at:at + size, q * 128:(q + 1) * 128]
        at += size


def class_bits(bits, c):
    if len(bits) == 2:
        return {bits[0]: c >> 1, bits[1]: c & 1}
    return {bits[0]: c}


def levels_kernel(levels, packed_in, x_ref, cos_ref, sin_ref, *refs):
    count_w = (len(refs) - 3) // 2
    m_refs = refs[:count_w]
    o_ref, s0, s1 = refs[count_w:count_w + 3]
    w_refs = refs[count_w + 3:]
    for w_ref, m_ref in zip(w_refs, m_refs):
        build_weights(w_ref, m_ref)
    rows = s0.shape[1]
    block = rows // 4
    if packed_in:
        whole = x_ref[...].astype(jnp.float32)
        lane = lax.broadcasted_iota(jnp.int32, (block, WIDE), 1)
        for b in range(4):
            piece = whole if b == 0 else pltpu.roll(whole, 4 * F - b * F, 1)
            piece = jnp.where(lane < F, piece[:, :WIDE], 0.0)
            for q in range(WIDE // 128):
                s0[q, b * block:(b + 1) * block, :] = piece[:, q * 128:(q + 1) * 128]
    else:
        for q in range(WIDE // 128):
            s0[q] = x_ref[:, q * 128:(q + 1) * 128].astype(jnp.float32)
    bufs = (s0, s1)
    for index, (kind, bits) in enumerate(levels):
        src = bufs[index % 2]
        dst = bufs[(index + 1) % 2]
        count = 4 if kind == "quad" else 2
        w_ref = w_refs[0] if kind == "quad" else w_refs[-1]
        children = [load_class(src, class_bits(bits, c)).astype(jnp.bfloat16) for c in range(count)]
        stacked = jnp.concatenate(children, 1)
        for t in range(count):
            fixed = class_bits(bits, t)
            y = lax.dot_general(
                stacked, w_ref[t], (((1,), (1,)), ((), ())), preferred_element_type=jnp.float32
            )
            lane = lax.broadcasted_iota(jnp.int32, y.shape, 1)
            swapped = jnp.where(lane < P_SIZE, pltpu.roll(y, WIDE - P_SIZE, 1), pltpu.roll(y, P_SIZE, 1))
            cs = load_class(cos_ref, fixed)
            sn = load_class(sin_ref, fixed)
            out = (y * cs + swapped * sn).astype(jnp.bfloat16).astype(jnp.float32)
            store_class(dst, fixed, out)
    last = bufs[len(levels) % 2]
    total = None
    pad = jnp.zeros((block, 4 * F - WIDE), jnp.float32)
    for b in range(4):
        piece = jnp.concatenate([last[q, b * block:(b + 1) * block, :] for q in range(WIDE // 128)], 1)
        piece = jnp.concatenate([piece, pad], 1)
        if b:
            piece = pltpu.roll(piece, b * F, 1)
        total = piece if total is None else total + piece
    o_ref[...] = total.astype(o_ref.dtype)


def run_levels(levels, packed_in, x, cos_t, sin_t, m_list):
    rows = 1024
    vmem = pl.BlockSpec(memory_space=pltpu.VMEM)
    w_scratch = [
        pltpu.VMEM((m.shape[0], WIDE, m.shape[1] * WIDE), jnp.bfloat16) for m in m_list
    ]
    m_list = [jnp.pad(m, [(0, 0)] * 4 + [(0, LANE - P_SIZE)]) for m in m_list]
    return pl.pallas_call(
        functools.partial(levels_kernel, levels, packed_in),
        out_shape=jax.ShapeDtypeStruct((rows // 4, 4 * F), jnp.bfloat16),
        in_specs=[vmem] * (3 + len(m_list)),
        out_specs=vmem,
        scratch_shapes=[pltpu.VMEM((WIDE // 128, rows, 128), jnp.float32)] * 2 + w_scratch,
        compiler_params=pltpu.CompilerParams(vmem_limit_bytes=60 * 1024 * 1024),
    )(x, cos_t, sin_t, *m_list)


def bits_of(value, count):
    return [(value >> k) & 1 for k in range(count)]


def tables(slope, a, b):
    center_x = (a.astype(jnp.float32) + 0.5) / 256.0 - 0.5
    center_y = (b.astype(jnp.float32) + 0.5) / 1024.0 - 0.5
    angle = slope[0][None, :] * center_x[:, None] + slope[1][None, :] * center_y[:, None]
    cosine = jnp.cos(angle)
    sine = jnp.sin(angle)
    pad = [(0, 0), (0, WIDE - F)]

    def chunked(v):
        return jnp.pad(v, pad).reshape(-1, WIDE // 128, 128).transpose(1, 0, 2)

    return chunked(jnp.concatenate([cosine, cosine], 1)), chunked(jnp.concatenate([-sine, sine], 1))


def exchange(z):
    shape = z.shape
    z = z.transpose(0, 1, 4, 2, 3, 5).reshape(shape[0] * shape[1], 2, -1)
    z = lax.all_to_all(z, ("gx", "gy"), 0, 0, tiled=True)
    z = z.reshape(shape[0], shape[1], 2, 2, 2, shape[5])
    return z.transpose(0, 1, 3, 4, 2, 5)


def local(source, slope, quad, pair):
    place_x = lax.axis_index("gx")
    place_y = lax.axis_index("gy")
    wq = quad.reshape(4, 4, 2, P_SIZE, P_SIZE)
    wp = pair.reshape(2, 2, 2, P_SIZE, P_SIZE)
    rows = jnp.arange(1024, dtype=jnp.int32)

    cos1, sin1 = tables(slope, place_x * 32 + (rows >> 5), place_y * 32 + (rows & 31))
    x = source.reshape(F, 1024).T
    x = jnp.pad(x, [(0, 0), (0, WIDE - F)])
    levels1 = [("quad", (k + 5, k)) for k in range(5)]
    y1 = run_levels(levels1, False, x, cos1, sin1, [wq])
    z = lax.all_to_all(y1, ("gx", "gy"), 0, 0, tiled=True)
    lo_a = place_x & 1
    lo_a = lo_a + 2 * ((place_x >> 1) & 1) + 4 * ((place_x >> 2) & 1)
    a2 = lo_a + 8 * ((rows >> 8) & 1) + 16 * ((rows >> 9) & 1) + 32 * ((rows >> 5) & 7)
    b2 = place_y + 32 * (rows & 31)
    cos2, sin2 = tables(slope, a2, b2)
    levels2 = [("quad", (5, 0)), ("quad", (6, 1)), ("quad", (7, 2)), ("pair", (3,)), ("pair", (4,))]
    y2 = run_levels(levels2, True, z, cos2, sin2, [wq, wp])
    w = lax.all_to_all(y2, ("gx", "gy"), 0, 0, tiled=True)
    w = w.reshape(256, 4, F).transpose(2, 1, 0)
    return w.reshape(F, 1, 1, 1024)


def solution(mesh):
    in_specs = (P(None, "gx", "gy", None), P(), P(), P())
    out_specs = P(None, "gx", "gy", None)
    return jax.shard_map(local, mesh=mesh, in_specs=in_specs, out_specs=out_specs, check_vma=False)
```

profile of v0, /device:TPU:1, one launch (start us, length us, event | category | flops | bytes accessed | tf_op | source)
XLA Modules:
  0.0 131.7 jit_solution(1671000226970693851)
XLA Ops:
  0.1 0.8 fusion.6
  0.8 5.4 %fusion.5 = (f32[1024,144]{0,1:T(8,128)}, f32[1024,144]{0,1:T(8,128)}, f32[1024,144]{0,1:T(8,128)}, f32[1024,144]{0,1:T(8,128)S(1)}, f32[1024,144]{0,1:T(8,128)S(1)}, /*index=5*/f32[1024,144]{0,1:T(8,128)S(1)}) fusion(f32[1024]{0:T(1024)S(1)} %multiply_add_fusion.2, f32[144]{0:T(256)S(1)} %bitcast.35, f32[1024]{0:T(1024)S(1)} %multiply_add_fusion.3, ...), kind=kLoop, calls=%fused_computation.13 | loop fusion | flops 1179648 | bytes 3556480 | tf_op jit(solution)/shard_map/neg | solution.py:171
  6.2 0.4 select_maximum_fusion.2
  6.6 1.7 %copy.30 = f32[1024,3,128]{2,0,1:T(8,128)} copy(f32[1024,3,128]{0,2,1:T(8,128)S(1)} %bitcast.27) | data formatting | bytes 3145728 | tf_op jit(solution)/shard_map/reshape | solution.py:169
  8.3 1.7 %copy.31 = f32[1024,3,128]{2,0,1:T(8,128)} copy(f32[1024,3,128]{0,2,1:T(8,128)S(1)} %bitcast.25) | data formatting | bytes 3145728 | tf_op jit(solution)/shard_map/reshape | solution.py:169
  9.9 5.7 %reshape.81 = bf16[4,4,2,144,144]{4,3,2,1,0:T(8,128)(2,1)S(1)} reshape(bf16[4,4,2,20736]{3,2,1,0:T(2,128)(2,1)} %param.6) | data formatting | bytes 2654208 | tf_op jit(solution)/shard_map/reshape | solution.py:185
  15.6 1.4 %copy.29 = bf16[288,1,1,1024]{0,3,2,1:T(8,128)(2,1)S(1)} copy(bf16[288,1,1,1024]{3,0,2,1:T(8,128)(2,1)} %param.4) | data formatting | bytes 1179648 | tf_op args[0]
  17.0 1.8 %pad.29.refs_0_ = bf16[4,4,2,144,256]{4,3,2,1,0:T(8,128)(2,1)} pad(bf16[4,4,2,144,144]{4,3,2,1,0:T(8,128)(2,1)S(1)} %reshape.81, bf16[]{:T(256)} %constant.13.clone.1), padding=0_0x0_0x0_0x0_0x0_112 | pad | bytes 3686402 | tf_op jit(solution)/shard_map/jit(_pad)/pad | solution.py:145
  18.9 1.0 pad.26.x_ref
  19.8 14.2 %shard_map.46 = bf16[256,1152]{1,0:T(8,128)(2,1)} custom-call(bf16[1024,384]{1,0:T(8,128)(2,1)} %pad.26.x_ref, f32[3,1024,128]{2,1,0:T(8,128)} %bitcast.23, f32[3,1024,128]{2,1,0:T(8,128)} %bitcast.24, bf16[4,4,2,144,256]{4,3,2,1,0:T(8,128)(2,1)} %pad.29.refs_0_), custom_call_target="tpu_custom_call" | custom-call | tf_op jit(solution)/shard_map/pallas_call | solution.py:146
  34.0 0.6 broadcast.215
  34.6 2.1 %reduce = bf16[256,1152]{1,0:T(8,128)(2,1)S(1)} reduce(bf16[256,1,1152]{2,0,1:T(8,128)(2,1)} %bitcast.33, bf16[]{:T(256)} %broadcast.215), dimensions={1}, to_apply=%copy.32.reduce_sub_computation | reduce | bytes 1179650 | tf_op jit(solution)/shard_map/all_to_all | solution.py:194
  36.7 1.5 %reshape.87 = bf16[256,2,576]{2,1,0:T(2,128)(2,1)} reshape(bf16[256,1152]{1,0:T(8,128)(2,1)S(1)} %reduce) | data formatting | bytes 1179648
  38.2 16.5 %all-to-all-start = ((bf16[256,2,576]{2,1,0:T(2,128)(2,1)}), bf16[256,2,576]{2,1,0:T(2,128)(2,1)}, u32[]{:S(2)}, u32[]{:S(2)}) async-start(bf16[256,2,576]{2,1,0:T(2,128)(2,1)} %reshape.87), calls=%async_computation | async-start | bytes 1310720 | tf_op jit(solution)/shard_map/all_to_all | solution.py:194
  54.8 2.0 %select_maximum_fusion = (f32[1024,384]{0,1:T(8,128)S(1)}, f32[1024,384]{0,1:T(8,128)S(1)}) fusion(f32[1024,144]{0,1:T(8,128)} %get-tuple-element.6, f32[1024,144]{0,1:T(8,128)} %get-tuple-element.5, f32[1024,144]{0,1:T(8,128)} %get-tuple-element.7), kind=kLoop, calls=%fused_computation | loop fusion | flops 2752512 | bytes 4915200 | tf_op jit(solution)/shard_map/concatenate | solution.py:171
  56.7 1.6 %copy.33 = f32[1024,3,128]{2,0,1:T(8,128)} copy(f32[1024,3,128]{0,2,1:T(8,128)S(1)} %bitcast.28) | data formatting | bytes 3145728 | tf_op jit(solution)/shard_map/reshape | solution.py:169
  58.3 0.0 copy-start
  58.3 1.6 %copy.34 = f32[1024,3,128]{2,0,1:T(8,128)} copy(f32[1024,3,128]{0,2,1:T(8,128)S(1)} %bitcast.26) | data formatting | bytes 3145728 | tf_op jit(solution)/shard_map/reshape | solution.py:169
  60.0 0.0 copy-done
  60.0 1.1 reshape.84
  61.1 0.9 pad.32.refs_1_
  62.0 14.8 %all-to-all-done = bf16[256,2,576]{2,1,0:T(2,128)(2,1)} async-done(((bf16[256,2,576]{2,1,0:T(2,128)(2,1)}), bf16[256,2,576]{2,1,0:T(2,128)(2,1)}, u32[]{:S(2)}, u32[]{:S(2)}) %all-to-all-start) | async-done | bytes 589856 | tf_op jit(solution)/shard_map/all_to_all | solution.py:194
  76.8 4.2 %reshape.88 = bf16[256,1,1152]{2,1,0:T(2,128)(2,1)S(1)} reshape(bf16[256,2,576]{2,1,0:T(2,128)(2,1)} %all-to-all-done) | data formatting | bytes 1179648
  81.0 0.9 copy.40
  81.8 13.2 %shard_map.47 = bf16[256,1152]{1,0:T(8,128)(2,1)} custom-call(bf16[256,1152]{1,0:T(8,128)(2,1)} %bitcast.30, f32[3,1024,128]{2,1,0:T(8,128)} %bitcast.21, f32[3,1024,128]{2,1,0:T(8,128)} %bitcast.22, bf16[4,4,2,144,256]{4,3,2,1,0:T(8,128)(2,1)} %pad.29.refs_0_, bf16[2,2,2,144,256]{4,3,2,1,0:T(8,128)(2,1)} %pad.32.refs_1_), custom_call_target="tpu_custom_call" | custom-call | tf_op jit(solution)/shard_map/pallas_call | solution.py:146
  95.1 2.1 %reduce.1 = bf16[256,1152]{1,0:T(8,128)(2,1)S(1)} reduce(bf16[256,1,1152]{2,0,1:T(8,128)(2,1)} %bitcast.31, bf16[]{:T(256)} %broadcast.215), dimensions={1}, to_apply=%copy.35.reduce_sub_computation | reduce | bytes 1179650 | tf_op jit(solution)/shard_map/all_to_all | solution.py:202
  97.2 0.6 reshape.89
  97.8 29.8 %all_to_all.20 = bf16[256,2,576]{2,1,0:T(2,128)(2,1)S(1)} all-to-all(bf16[256,2,576]{2,1,0:T(2,128)(2,1)S(1)} %reshape.89), channel_id=1, replica_groups=mesh['gx'=8,'gy'=32] {'gx','gy'}, dimensions={0} | all-to-all | bytes 1179648 | tf_op jit(solution)/shard_map/all_to_all | solution.py:202
  127.7 1.0 reshape.90
  128.7 1.3 %copy.36 = bf16[256,1,1152]{0,2,1:T(8,128)(2,1)S(1)} copy(bf16[256,1,1152]{2,1,0:T(2,128)(2,1)S(1)} %reshape.90) | data formatting | bytes 1179648 | tf_op jit(solution)/shard_map/all_to_all | solution.py:202
  130.0 0.5 copy.37
  130.5 1.2 reshape.86
  (4 shorter events, 0.0 us)
Async XLA Ops:
  38.2 38.5 %all-to-all-start = ((bf16[256,2,576]{2,1,0:T(2,128)(2,1)}), bf16[256,2,576]{2,1,0:T(2,128)(2,1)}, u32[]{:S(2)}, u32[]{:S(2)}) async-start(bf16[256,2,576]{2,1,0:T(2,128)(2,1)} %reshape.87), calls=%async_computation | async-start | bytes 1310720 | tf_op jit(solution)/shard_map/all_to_all | solution.py:194
  58.3 1.6 %copy-start = (bf16[2,2,2,20736]{3,2,1,0:T(2,128)(2,1)S(1)}, bf16[2,2,2,20736]{3,2,1,0:T(2,128)(2,1)}, u32[]{:S(2)}) copy-start(bf16[2,2,2,20736]{3,2,1,0:T(2,128)(2,1)} %param.7) | copy-start | bytes 995332
where the time goes:
time: 132 us
  local copies, waits for them, and re-layouts  31 us (23%)
  blocking collectives  29.8 us (23%)
  Pallas kernels  27.4 us (21%)
  starting transfers between devices  16.5 us (12%)
  waiting for transfers between devices  14.8 us (11%)
  other arithmetic  12 us (9%)
    all_to_all x1, blocking collectives, local(): w = lax.all_to_all(y2, ('gx', 'gy'), 0, 0, tiled=True)  29.8 us
    pallas_call x2, Pallas kernels, run_levels(): pl.pallas_call(functools.partial(levels_kernel, levels, packed_in), out_s...  27.4 us
    all_to_all x1, starting transfers between devices, local(): z = lax.all_to_all(y1, ('gx', 'gy'), 0, 0, tiled=True)  16.5 us
    all_to_all x1, waiting for transfers between devices, local(): z = lax.all_to_all(y1, ('gx', 'gy'), 0, 0, tiled=True)  14.8 us
    unnamed x8, local copies, waits for them, and re-layouts  9.59 us
    reshape x4, local copies, waits for them, and re-layouts, chunked(): return jnp.pad(v, pad).reshape(-1, WIDE // 128, 128).transpose(1, 0, 2)  6.58 us
    reshape x1, local copies, waits for them, and re-layouts, local(): wq = quad.reshape(4, 4, 2, P_SIZE, P_SIZE)  5.66 us
    neg x1, other arithmetic, tables(): -sine  5.4 us
  transfers between devices with their start and end apart: 1, of which 1 were waited for; matrix products, arithmetic and copies ran while one was open for 5% of the time, Pallas kernels for 0%

commit v1 on v0

--- a/solution.py
+++ b/solution.py
@@ -85,11 +85,12 @@
     return {bits[0]: c}
 
 
-def levels_kernel(levels, packed_in, x_ref, cos_ref, sin_ref, *refs):
-    count_w = (len(refs) - 3) // 2
+def levels_kernel(levels, packed_in, x_ref, f_ref, *refs):
+    count_w = (len(refs) - 5) // 2
     m_refs = refs[:count_w]
-    o_ref, s0, s1 = refs[count_w:count_w + 3]
-    w_refs = refs[count_w + 3:]
+    o_ref, s0, s1, cos_ref, sin_ref = refs[count_w:count_w + 5]
+    w_refs = refs[count_w + 5:]
+    build_tables(cos_ref, sin_ref, f_ref)
     for w_ref, m_ref in zip(w_refs, m_refs):
         build_weights(w_ref, m_ref)
     rows = s0.shape[1]
@@ -136,7 +137,7 @@
     o_ref[...] = total.astype(o_ref.dtype)
 
 
-def run_levels(levels, packed_in, x, cos_t, sin_t, m_list):
+def run_levels(levels, packed_in, x, f_t, m_list):
     rows = 1024
     vmem = pl.BlockSpec(memory_space=pltpu.VMEM)
     w_scratch = [
@@ -146,29 +147,45 @@
     return pl.pallas_call(
         functools.partial(levels_kernel, levels, packed_in),
         out_shape=jax.ShapeDtypeStruct((rows // 4, 4 * F), jnp.bfloat16),
-        in_specs=[vmem] * (3 + len(m_list)),
+        in_specs=[vmem] * (2 + len(m_list)),
         out_specs=vmem,
-        scratch_shapes=[pltpu.VMEM((WIDE // 128, rows, 128), jnp.float32)] * 2 + w_scratch,
+        scratch_shapes=[pltpu.VMEM((WIDE // 128, rows, 128), jnp.float32)] * 4 + w_scratch,
         compiler_params=pltpu.CompilerParams(vmem_limit_bytes=60 * 1024 * 1024),
-    )(x, cos_t, sin_t, *m_list)
+    )(x, f_t, *m_list)
 
 
 def bits_of(value, count):
     return [(value >> k) & 1 for k in range(count)]
 
 
-def tables(slope, a, b):
+def factors(slope, a, b):
     center_x = (a.astype(jnp.float32) + 0.5) / 256.0 - 0.5
     center_y = (b.astype(jnp.float32) + 0.5) / 1024.0 - 0.5
-    angle = slope[0][None, :] * center_x[:, None] + slope[1][None, :] * center_y[:, None]
-    cosine = jnp.cos(angle)
-    sine = jnp.sin(angle)
+    part_a = slope[0][None, :] * center_x[:, None]
+    part_b = slope[1][None, :] * center_y[:, None]
     pad = [(0, 0), (0, WIDE - F)]
 
-    def chunked(v):
-        return jnp.pad(v, pad).reshape(-1, WIDE // 128, 128).transpose(1, 0, 2)
-
-    return chunked(jnp.concatenate([cosine, cosine], 1)), chunked(jnp.concatenate([-sine, sine], 1))
+    def lanes(v):
+        return jnp.pad(jnp.concatenate([v, v], 1), pad)
+
+    return jnp.stack([lanes(jnp.cos(part_a)), lanes(jnp.sin(part_a)), lanes(jnp.cos(part_b)), lanes(jnp.sin(part_b))])
+
+
+def build_tables(cos_ref, sin_ref, f_ref):
+    groups = f_ref.shape[1]
+    cb = f_ref[2]
+    sb = f_ref[3]
+    lane = lax.broadcasted_iota(jnp.int32, cb.shape, 1)
+    for i in range(groups):
+        ca = f_ref[0, i:i + 1, :]
+        sa = f_ref[1, i:i + 1, :]
+        cosine = ca * cb - sa * sb
+        sine = sa * cb + ca * sb
+        sine = jnp.where(lane < P_SIZE, -sine, sine)
+        rows = pl.ds(i * groups, groups)
+        for q in range(WIDE // 128):
+            cos_ref[q, rows, :] = cosine[:, q * 128:(q + 1) * 128]
+            sin_ref[q, rows, :] = sine[:, q * 128:(q + 1) * 128]
 
 
 def exchange(z):
@@ -184,21 +201,19 @@
     place_y = lax.axis_index("gy")
     wq = quad.reshape(4, 4, 2, P_SIZE, P_SIZE)
     wp = pair.reshape(2, 2, 2, P_SIZE, P_SIZE)
-    rows = jnp.arange(1024, dtype=jnp.int32)
-
-    cos1, sin1 = tables(slope, place_x * 32 + (rows >> 5), place_y * 32 + (rows & 31))
+    group = jnp.arange(32, dtype=jnp.int32)
+
+    f1 = factors(slope, place_x * 32 + group, place_y * 32 + group)
     x = source.reshape(F, 1024).T
     x = jnp.pad(x, [(0, 0), (0, WIDE - F)])
     levels1 = [("quad", (k + 5, k)) for k in range(5)]
-    y1 = run_levels(levels1, False, x, cos1, sin1, [wq])
+    y1 = run_levels(levels1, False, x, f1, [wq])
     z = lax.all_to_all(y1, ("gx", "gy"), 0, 0, tiled=True)
-    lo_a = place_x & 1
-    lo_a = lo_a + 2 * ((place_x >> 1) & 1) + 4 * ((place_x >> 2) & 1)
-    a2 = lo_a + 8 * ((rows >> 8) & 1) + 16 * ((rows >> 9) & 1) + 32 * ((rows >> 5) & 7)
-    b2 = place_y + 32 * (rows & 31)
-    cos2, sin2 = tables(slope, a2, b2)
+    a2 = place_x + 8 * ((group >> 3) & 1) + 16 * ((group >> 4) & 1) + 32 * (group & 7)
+    b2 = place_y + 32 * group
+    f2 = factors(slope, a2, b2)
     levels2 = [("quad", (5, 0)), ("quad", (6, 1)), ("quad", (7, 2)), ("pair", (3,)), ("pair", (4,))]
-    y2 = run_levels(levels2, True, z, cos2, sin2, [wq, wp])
+    y2 = run_levels(levels2, True, z, f2, [wq, wp])
     w = lax.all_to_all(y2, ("gx", "gy"), 0, 0, tiled=True)
     w = w.reshape(256, 4, F).transpose(2, 1, 0)
     return w.reshape(F, 1, 1, 1024)

time: 132 us -> 119 us (0.902)
  local copies, waits for them, and re-layouts: 31 us -> 21 us
  other arithmetic: 12 us -> 6.33 us
  waiting for transfers between devices: 14.8 us -> 19.9 us
  Pallas kernels: 27.4 us -> 26 us
    reshape x4 -> x0, local copies, waits for them, and re-layouts: 6.58 us -> none  [chunked(): return jnp.pad(v, pad).reshape(-1, WIDE // 128, 128).transpose(1, 0, 2)]
    neg x1 -> x0, other arithmetic: 5.4 us -> none  [tables(): -sine]
    all_to_all x1, waiting for transfers between devices: 14.8 us -> 19.9 us  [local(): z = lax.all_to_all(y1, ('gx', 'gy'), 0, 0, tiled=True)]
    unnamed x8, local copies, waits for them, and re-layouts: 9.59 us -> 6.4 us
    concatenate x2 -> x0, other arithmetic: 2.32 us -> none  [tables(): jnp.concatenate([-sine, sine], 1)]
    another operation x0 -> x6, other arithmetic: none -> 1.71 us  [factors(): jnp.stack([lanes(jnp.cos(part_a)), lanes(jnp.sin(part_a)), lanes(jnp.cos(...]
    pallas_call x2, Pallas kernels: 27.4 us -> 26 us  [run_levels(): pl.pallas_call(functools.partial(levels_kernel, levels, packed_in), out_s...]
  transfers between devices with their start and end apart: 1 -> 1, of which waited for: 1 -> 1; matrix products, arithmetic and copies ran while one was open for 5% -> 2% of each run, Pallas kernels for 0% -> 0%
where the time goes in v1:
time: 119 us
  blocking collectives  29.8 us (25%)
  Pallas kernels  26 us (22%)
  local copies, waits for them, and re-layouts  21 us (18%)
  waiting for transfers between devices  19.9 us (17%)
  starting transfers between devices  15.7 us (13%)
  other arithmetic  6.33 us (5%)
    all_to_all x1, blocking collectives, local(): w = lax.all_to_all(y2, ('gx', 'gy'), 0, 0, tiled=True)  29.8 us
    pallas_call x2, Pallas kernels, run_levels(): pl.pallas_call(functools.partial(levels_kernel, levels, packed_in), out_s...  26 us
    all_to_all x1, waiting for transfers between devices, local(): z = lax.all_to_all(y1, ('gx', 'gy'), 0, 0, tiled=True)  19.9 us
    all_to_all x1, starting transfers between devices, local(): z = lax.all_to_all(y1, ('gx', 'gy'), 0, 0, tiled=True)  15.7 us
    unnamed x8, local copies, waits for them, and re-layouts  6.4 us
    reshape x1, local copies, waits for them, and re-layouts, local(): wq = quad.reshape(4, 4, 2, P_SIZE, P_SIZE)  5.48 us
    pad x2, local copies, waits for them, and re-layouts, run_levels(): m_list = [jnp.pad(m, [(0, 0)] * 4 + [(0, LANE - P_SIZE)]) for m in m_list]  2.77 us
  transfers between devices with their start and end apart: 1, of which 1 were waited for; matrix products, arithmetic and copies ran while one was open for 2% of the time, Pallas kernels for 0%

profile of v1, /device:TPU:1, one launch (start us, length us, event | category | flops | bytes accessed | tf_op | source)
XLA Modules:
  0.0 118.8 jit_solution(15063495419328107315)
XLA Ops:
  0.0 0.8 fusion.8
  0.8 5.5 %reshape.66 = bf16[4,4,2,144,144]{4,3,2,1,0:T(8,128)(2,1)S(1)} reshape(bf16[4,4,2,20736]{3,2,1,0:T(2,128)(2,1)} %param.6) | data formatting | bytes 2654208 | tf_op jit(solution)/shard_map/reshape | solution.py:202
  6.3 1.4 %copy.17 = bf16[288,1,1,1024]{0,3,2,1:T(8,128)(2,1)S(1)} copy(bf16[288,1,1,1024]{3,0,2,1:T(8,128)(2,1)} %param.4) | data formatting | bytes 1179648 | tf_op args[0]
  7.7 1.8 %pad.43.refs_0_ = bf16[4,4,2,144,256]{4,3,2,1,0:T(8,128)(2,1)} pad(bf16[4,4,2,144,144]{4,3,2,1,0:T(8,128)(2,1)S(1)} %reshape.66, bf16[]{:T(256)} %constant.13.clone.1), padding=0_0x0_0x0_0x0_0x0_112 | pad | bytes 3686402 | tf_op jit(solution)/shard_map/jit(_pad)/pad | solution.py:146
  9.6 1.0 pad.38.x_ref
  10.6 0.3 multiply_cosine_fusion.1
  10.9 0.1 fusion.6
  11.0 0.3 multiply_cosine_fusion
  11.3 0.1 fusion.4
  11.4 0.7 pad_maximum_fusion.f_ref
  12.1 13.4 %shard_map.46 = bf16[256,1152]{1,0:T(8,128)(2,1)} custom-call(bf16[1024,384]{1,0:T(8,128)(2,1)} %pad.38.x_ref, f32[4,32,384]{2,1,0:T(8,128)} %pad_maximum_fusion.f_ref, bf16[4,4,2,144,256]{4,3,2,1,0:T(8,128)(2,1)} %pad.43.refs_0_), custom_call_target="tpu_custom_call" | custom-call | tf_op jit(solution)/shard_map/pallas_call | solution.py:147
  25.5 0.5 broadcast.216
  25.9 2.0 %reduce = bf16[256,1152]{1,0:T(8,128)(2,1)S(1)} reduce(bf16[256,1,1152]{2,0,1:T(8,128)(2,1)} %bitcast.33, bf16[]{:T(256)} %broadcast.216), dimensions={1}, to_apply=%copy.18.reduce_sub_computation | reduce | bytes 1179650 | tf_op jit(solution)/shard_map/all_to_all | solution.py:211
  27.9 0.0 copy-start
  27.9 1.5 %reshape.70 = bf16[256,2,576]{2,1,0:T(2,128)(2,1)} reshape(bf16[256,1152]{1,0:T(8,128)(2,1)S(1)} %reduce) | data formatting | bytes 1179648
  29.4 15.7 %all-to-all-start = ((bf16[256,2,576]{2,1,0:T(2,128)(2,1)}), bf16[256,2,576]{2,1,0:T(2,128)(2,1)S(1)}, u32[]{:S(2)}, u32[]{:S(2)}) async-start(bf16[256,2,576]{2,1,0:T(2,128)(2,1)} %reshape.70), calls=%async_computation | async-start | bytes 1310720 | tf_op jit(solution)/shard_map/all_to_all | solution.py:211
  45.1 0.0 copy-done
  45.1 1.1 reshape.67
  46.2 0.9 pad.48.refs_1_
  47.1 0.1 fusion.2
  47.2 0.1 fusion
  47.3 0.7 pad_maximum_fusion.1.f_ref
  48.0 19.9 %all-to-all-done = bf16[256,2,576]{2,1,0:T(2,128)(2,1)S(1)} async-done(((bf16[256,2,576]{2,1,0:T(2,128)(2,1)}), bf16[256,2,576]{2,1,0:T(2,128)(2,1)S(1)}, u32[]{:S(2)}, u32[]{:S(2)}) %all-to-all-start) | async-done | bytes 589856 | tf_op jit(solution)/shard_map/all_to_all | solution.py:211
  67.9 1.0 reshape.71
  68.9 0.9 copy.24
  69.7 12.6 %shard_map.47 = bf16[256,1152]{1,0:T(8,128)(2,1)} custom-call(bf16[256,1152]{1,0:T(8,128)(2,1)} %bitcast.31, f32[4,32,384]{2,1,0:T(8,128)} %pad_maximum_fusion.1.f_ref, bf16[4,4,2,144,256]{4,3,2,1,0:T(8,128)(2,1)} %pad.43.refs_0_, bf16[2,2,2,144,256]{4,3,2,1,0:T(8,128)(2,1)} %pad.48.refs_1_), custom_call_target="tpu_custom_call" | custom-call | tf_op jit(solution)/shard_map/pallas_call | solution.py:147
  82.3 2.0 %reduce.1 = bf16[256,1152]{1,0:T(8,128)(2,1)S(1)} reduce(bf16[256,1,1152]{2,0,1:T(8,128)(2,1)} %bitcast.32, bf16[]{:T(256)} %broadcast.216), dimensions={1}, to_apply=%copy.19.reduce_sub_computation | reduce | bytes 1179650 | tf_op jit(solution)/shard_map/all_to_all | solution.py:217
  84.3 0.6 reshape.72
  84.9 29.8 %all_to_all.20 = bf16[256,2,576]{2,1,0:T(2,128)(2,1)S(1)} all-to-all(bf16[256,2,576]{2,1,0:T(2,128)(2,1)S(1)} %reshape.72), channel_id=1, replica_groups=mesh['gx'=8,'gy'=32] {'gx','gy'}, dimensions={0} | all-to-all | bytes 1179648 | tf_op jit(solution)/shard_map/all_to_all | solution.py:217
  114.7 1.0 reshape.73
  115.7 1.3 %copy.20 = bf16[256,1,1152]{0,2,1:T(8,128)(2,1)S(1)} copy(bf16[256,1,1152]{2,1,0:T(2,128)(2,1)S(1)} %reshape.73) | data formatting | bytes 1179648 | tf_op jit(solution)/shard_map/all_to_all | solution.py:217
  117.1 0.5 copy.21
  117.5 1.2 %reshape.69 = bf16[288,1,1,1024]{3,0,2,1:T(8,128)(2,1)} reshape(bf16[288,4,256]{2,1,0:T(4,128)(2,1)S(1)} %copy.21) | data formatting | bytes 1179648 | tf_op jit(solution)/shard_map/reshape | solution.py:219
  (4 shorter events, 0.0 us)
Async XLA Ops:
  27.9 17.2 %copy-start = (bf16[2,2,2,20736]{3,2,1,0:T(2,128)(2,1)S(1)}, bf16[2,2,2,20736]{3,2,1,0:T(2,128)(2,1)}, u32[]{:S(2)}) copy-start(bf16[2,2,2,20736]{3,2,1,0:T(2,128)(2,1)} %param.7) | copy-start | bytes 995332
  29.4 38.4 %all-to-all-start = ((bf16[256,2,576]{2,1,0:T(2,128)(2,1)}), bf16[256,2,576]{2,1,0:T(2,128)(2,1)S(1)}, u32[]{:S(2)}, u32[]{:S(2)}) async-start(bf16[256,2,576]{2,1,0:T(2,128)(2,1)} %reshape.70), calls=%async_computation | async-start | bytes 1310720 | tf_op jit(solution)/shard_map/all_to_all | solution.py:211

commit v2 on v1

--- a/solution.py
+++ b/solution.py
@@ -196,6 +196,18 @@
     return z.transpose(0, 1, 3, 4, 2, 5)
 
 
+def exchange2(y):
+    lanes = y.shape[1]
+    cut = 512
+    first = y[:, :cut].reshape(8, 32, cut)
+    second = y[:, cut:].reshape(8, 32, lanes - cut)
+    first = lax.all_to_all(first, "gx", 0, 0, tiled=True)
+    second = lax.all_to_all(second, "gy", 1, 1, tiled=True)
+    first = lax.all_to_all(first, "gy", 1, 1, tiled=True)
+    second = lax.all_to_all(second, "gx", 0, 0, tiled=True)
+    return jnp.concatenate([first.reshape(256, cut), second.reshape(256, lanes - cut)], 1)
+
+
 def local(source, slope, quad, pair):
     place_x = lax.axis_index("gx")
     place_y = lax.axis_index("gy")
@@ -208,13 +220,13 @@
     x = jnp.pad(x, [(0, 0), (0, WIDE - F)])
     levels1 = [("quad", (k + 5, k)) for k in range(5)]
     y1 = run_levels(levels1, False, x, f1, [wq])
-    z = lax.all_to_all(y1, ("gx", "gy"), 0, 0, tiled=True)
+    z = exchange2(y1)
     a2 = place_x + 8 * ((group >> 3) & 1) + 16 * ((group >> 4) & 1) + 32 * (group & 7)
     b2 = place_y + 32 * group
     f2 = factors(slope, a2, b2)
     levels2 = [("quad", (5, 0)), ("quad", (6, 1)), ("quad", (7, 2)), ("pair", (3,)), ("pair", (4,))]
     y2 = run_levels(levels2, True, z, f2, [wq, wp])
-    w = lax.all_to_all(y2, ("gx", "gy"), 0, 0, tiled=True)
+    w = exchange2(y2)
     w = w.reshape(256, 4, F).transpose(2, 1, 0)
     return w.reshape(F, 1, 1, 1024)
 

time: 119 us -> 174 us (1.46)
  waiting for transfers between devices: 19.9 us -> 72.6 us
  starting transfers between devices: 15.7 us -> 47.1 us
  blocking collectives: 29.8 us -> 0 us
  other arithmetic: 6.33 us -> 3.28 us
  local copies, waits for them, and re-layouts: 21 us -> 22.9 us
    all_to_all x1 -> x8, waiting for transfers between devices: 19.9 us -> 72.6 us  [the longest x2 27.4 us: exchange2(): second = lax.all_to_all(second, 'gy', 1, 1, tiled=True)]
    all_to_all x1 -> x8, starting transfers between devices: 15.7 us -> 47.1 us  [the longest x2 20.3 us: exchange2(): second = lax.all_to_all(second, 'gy', 1, 1, tiled=True)]
    all_to_all x1 -> x0, blocking collectives: 29.8 us -> none  [local(): w = lax.all_to_all(y2, ('gx', 'gy'), 0, 0, tiled=True)]
    unnamed x8 -> x3, local copies, waits for them, and re-layouts: 6.4 us -> 1.43 us
    all_to_all x2 -> x0, other arithmetic: 3.96 us -> none  [the longest x1 1.98 us: local(): z = lax.all_to_all(y1, ('gx', 'gy'), 0, 0, tiled=True)]
    slice x0 -> x6, local copies, waits for them, and re-layouts: none -> 3.44 us  [the longest x2 3.43 us: exchange2(): first = y[:, :cut].reshape(8, 32, cut)]
  transfers between devices with their start and end apart: 1 -> 8, of which waited for: 1 -> 8; matrix products, arithmetic and copies ran while one was open for 2% -> 5% of each run, Pallas kernels for 0% -> 0%
where the time goes in v2:
time: 174 us; the launch traced here: 172 us
  waiting for transfers between devices  72.6 us (42%)
  starting transfers between devices  47.1 us (27%)
  Pallas kernels  26 us (15%)
  local copies, waits for them, and re-layouts  22.9 us (13%)
  other arithmetic  3.28 us (2%)
    all_to_all x2, waiting for transfers between devices, exchange2(): second = lax.all_to_all(second, 'gy', 1, 1, tiled=True)  27.4 us
    pallas_call x2, Pallas kernels, run_levels(): pl.pallas_call(functools.partial(levels_kernel, levels, packed_in), out_s...  26 us
    all_to_all x2, waiting for transfers between devices, exchange2(): first = lax.all_to_all(first, 'gy', 1, 1, tiled=True)  25.3 us
    all_to_all x2, starting transfers between devices, exchange2(): second = lax.all_to_all(second, 'gy', 1, 1, tiled=True)  20.3 us
    all_to_all x2, starting transfers between devices, exchange2(): first = lax.all_to_all(first, 'gy', 1, 1, tiled=True)  10.6 us
    all_to_all x2, waiting for transfers between devices, exchange2(): first = lax.all_to_all(first, 'gx', 0, 0, tiled=True)  10.4 us
    all_to_all x2, waiting for transfers between devices, exchange2(): second = lax.all_to_all(second, 'gx', 0, 0, tiled=True)  9.47 us
    all_to_all x2, starting transfers between devices, exchange2(): first = lax.all_to_all(first, 'gx', 0, 0, tiled=True)  9.35 us
  transfers between devices with their start and end apart: 8, of which 8 were waited for; matrix products, arithmetic and copies ran while one was open for 5% of the time, Pallas kernels for 0%

profile of v2, /device:TPU:1, one launch (start us, length us, event | category | flops | bytes accessed | tf_op | source)
XLA Modules:
  0.0 172.2 jit_solution(5701192779506374783)
XLA Ops:
  0.0 0.8 fusion.8
  0.8 5.5 %reshape.85 = bf16[4,4,2,144,144]{4,3,2,1,0:T(8,128)(2,1)S(1)} reshape(bf16[4,4,2,20736]{3,2,1,0:T(2,128)(2,1)} %param.6) | data formatting | bytes 2654208 | tf_op jit(solution)/shard_map/reshape | solution.py:214
  6.3 1.4 copy.23
  7.7 1.9 %pad.43.refs_0_ = bf16[4,4,2,144,256]{4,3,2,1,0:T(8,128)(2,1)} pad(bf16[4,4,2,144,144]{4,3,2,1,0:T(8,128)(2,1)S(1)} %reshape.85, bf16[]{:T(256)} %constant.13.clone.1), padding=0_0x0_0x0_0x0_0x0_112 | pad | bytes 3686402 | tf_op jit(solution)/shard_map/jit(_pad)/pad | solution.py:146
  9.6 1.0 pad.38.x_ref
  10.6 0.3 multiply_cosine_fusion.1
  10.9 0.1 fusion.6
  11.0 0.3 multiply_cosine_fusion
  11.3 0.1 fusion.4
  11.4 0.7 pad_maximum_fusion.2.f_ref
  12.1 13.4 %shard_map.46 = bf16[256,1152]{1,0:T(8,128)(2,1)} custom-call(bf16[1024,384]{1,0:T(8,128)(2,1)} %pad.38.x_ref, f32[4,32,384]{2,1,0:T(8,128)} %pad_maximum_fusion.2.f_ref, bf16[4,4,2,144,256]{4,3,2,1,0:T(8,128)(2,1)} %pad.43.refs_0_), custom_call_target="tpu_custom_call" | custom-call | tf_op jit(solution)/shard_map/pallas_call | solution.py:147
  25.5 0.0 slice-start.1
  25.5 1.7 slice.26
  27.2 5.9 %all-to-all-start = ((bf16[8,32,512]{2,1,0:T(8,128)(2,1)}), bf16[8,32,512]{2,1,0:T(8,128)(2,1)S(1)}, u32[]{:S(2)}, u32[]{:S(2)}) async-start(bf16[8,32,512]{2,1,0:T(8,128)(2,1)} %bitcast.8), calls=%async_computation | async-start | bytes 524288 | tf_op jit(solution)/shard_map/all_to_all | solution.py:204
  33.1 0.0 slice-done.1
  33.1 0.8 copy.26
  34.0 5.3 %all-to-all-done = bf16[8,32,512]{2,1,0:T(8,128)(2,1)S(1)} async-done(((bf16[8,32,512]{2,1,0:T(8,128)(2,1)}), bf16[8,32,512]{2,1,0:T(8,128)(2,1)S(1)}, u32[]{:S(2)}, u32[]{:S(2)}) %all-to-all-start) | async-done | bytes 262176 | tf_op jit(solution)/shard_map/all_to_all | solution.py:204
  39.2 12.9 %all-to-all-start.2 = ((bf16[8,32,640]{2,0,1:T(8,128)(2,1)}), bf16[8,32,640]{2,0,1:T(8,128)(2,1)S(1)}, u32[]{:S(2)}, u32[]{:S(2)}) async-start(bf16[8,32,640]{2,0,1:T(8,128)(2,1)} %copy.26), calls=%async_computation.2 | async-start | bytes 655360 | tf_op jit(solution)/shard_map/all_to_all | solution.py:205
  52.1 0.0 copy-start
  52.1 0.9 copy.24
  53.0 13.6 %all-to-all-done.2 = bf16[8,32,640]{2,0,1:T(8,128)(2,1)S(1)} async-done(((bf16[8,32,640]{2,0,1:T(8,128)(2,1)}), bf16[8,32,640]{2,0,1:T(8,128)(2,1)S(1)}, u32[]{:S(2)}, u32[]{:S(2)}) %all-to-all-start.2) | async-done | bytes 327712 | tf_op jit(solution)/shard_map/all_to_all | solution.py:205
  66.6 5.4 %all-to-all-start.1 = ((bf16[8,32,512]{2,0,1:T(8,128)(2,1)}), bf16[8,32,512]{2,0,1:T(8,128)(2,1)S(1)}, u32[]{:S(2)}, u32[]{:S(2)}) async-start(bf16[8,32,512]{2,0,1:T(8,128)(2,1)} %copy.24), calls=%async_computation.1 | async-start | bytes 524288 | tf_op jit(solution)/shard_map/all_to_all | solution.py:206
  72.1 0.8 copy.27
  72.8 12.6 %all-to-all-done.1 = bf16[8,32,512]{2,0,1:T(8,128)(2,1)S(1)} async-done(((bf16[8,32,512]{2,0,1:T(8,128)(2,1)}), bf16[8,32,512]{2,0,1:T(8,128)(2,1)S(1)}, u32[]{:S(2)}, u32[]{:S(2)}) %all-to-all-start.1) | async-done | bytes 262176 | tf_op jit(solution)/shard_map/all_to_all | solution.py:206
  85.5 3.4 %all-to-all-start.3 = ((bf16[8,32,640]{2,1,0:T(8,128)(2,1)}), bf16[8,32,640]{2,1,0:T(8,128)(2,1)S(1)}, u32[]{:S(2)}, u32[]{:S(2)}) async-start(bf16[8,32,640]{2,1,0:T(8,128)(2,1)} %copy.27), calls=%async_computation.3 | async-start | bytes 655360 | tf_op jit(solution)/shard_map/all_to_all | solution.py:207
  88.9 0.1 fusion.2
  89.0 0.0 copy-done
  89.0 1.1 reshape.90
  90.1 0.9 pad.48.refs_1_
  91.0 0.1 fusion
  91.1 0.7 pad_maximum_fusion.3.f_ref
  91.8 0.1 copy.25
  91.9 3.3 %all-to-all-done.3 = bf16[8,32,640]{2,1,0:T(8,128)(2,1)S(1)} async-done(((bf16[8,32,640]{2,1,0:T(8,128)(2,1)}), bf16[8,32,640]{2,1,0:T(8,128)(2,1)S(1)}, u32[]{:S(2)}, u32[]{:S(2)}) %all-to-all-start.3) | async-done | bytes 327712 | tf_op jit(solution)/shard_map/all_to_all | solution.py:207
  95.2 0.9 pad_maximum_fusion.x_ref
  96.0 12.6 %shard_map.47 = bf16[256,1152]{1,0:T(8,128)(2,1)} custom-call(bf16[256,1152]{1,0:T(8,128)(2,1)} %pad_maximum_fusion.x_ref, f32[4,32,384]{2,1,0:T(8,128)} %pad_maximum_fusion.3.f_ref, bf16[4,4,2,144,256]{4,3,2,1,0:T(8,128)(2,1)} %pad.43.refs_0_, bf16[2,2,2,144,256]{4,3,2,1,0:T(8,128)(2,1)} %pad.48.refs_1_), custom_call_target="tpu_custom_call" | custom-call | tf_op jit(solution)/shard_map/pallas_call | solution.py:147
  108.6 0.0 slice-start
  108.6 1.7 slice.28
  110.3 3.4 %all-to-all-start.4 = ((bf16[8,32,512]{2,1,0:T(8,128)(2,1)}), bf16[8,32,512]{2,1,0:T(8,128)(2,1)S(1)}, u32[]{:S(2)}, u32[]{:S(2)}) async-start(bf16[8,32,512]{2,1,0:T(8,128)(2,1)} %bitcast.16), calls=%async_computation.4 | async-start | bytes 524288 | tf_op jit(solution)/shard_map/all_to_all | solution.py:204
  113.8 0.0 slice-done
  113.8 0.8 copy.30
  114.6 5.2 %all-to-all-done.4 = bf16[8,32,512]{2,1,0:T(8,128)(2,1)S(1)} async-done(((bf16[8,32,512]{2,1,0:T(8,128)(2,1)}), bf16[8,32,512]{2,1,0:T(8,128)(2,1)S(1)}, u32[]{:S(2)}, u32[]{:S(2)}) %all-to-all-start.4) | async-done | bytes 262176 | tf_op jit(solution)/shard_map/all_to_all | solution.py:204
  119.8 7.4 %all-to-all-start.6 = ((bf16[8,32,640]{2,0,1:T(8,128)(2,1)}), bf16[8,32,640]{2,0,1:T(8,128)(2,1)S(1)}, u32[]{:S(2)}, u32[]{:S(2)}) async-start(bf16[8,32,640]{2,0,1:T(8,128)(2,1)} %copy.30), calls=%async_computation.6 | async-start | bytes 655360 | tf_op jit(solution)/shard_map/all_to_all | solution.py:205
  127.2 0.8 copy.28
  128.0 13.8 %all-to-all-done.6 = bf16[8,32,640]{2,0,1:T(8,128)(2,1)S(1)} async-done(((bf16[8,32,640]{2,0,1:T(8,128)(2,1)}), bf16[8,32,640]{2,0,1:T(8,128)(2,1)S(1)}, u32[]{:S(2)}, u32[]{:S(2)}) %all-to-all-start.6) | async-done | bytes 327712 | tf_op jit(solution)/shard_map/all_to_all | solution.py:205
  141.8 5.2 %all-to-all-start.5 = ((bf16[8,32,512]{2,0,1:T(8,128)(2,1)}), bf16[8,32,512]{2,0,1:T(8,128)(2,1)S(1)}, u32[]{:S(2)}, u32[]{:S(2)}) async-start(bf16[8,32,512]{2,0,1:T(8,128)(2,1)} %copy.28), calls=%async_computation.5 | async-start | bytes 524288 | tf_op jit(solution)/shard_map/all_to_all | solution.py:206
  147.1 0.8 copy.31
  147.8 12.6 %all-to-all-done.5 = bf16[8,32,512]{2,0,1:T(8,128)(2,1)S(1)} async-done(((bf16[8,32,512]{2,0,1:T(8,128)(2,1)}), bf16[8,32,512]{2,0,1:T(8,128)(2,1)S(1)}, u32[]{:S(2)}, u32[]{:S(2)}) %all-to-all-start.5) | async-done | bytes 262176 | tf_op jit(solution)/shard_map/all_to_all | solution.py:206
  160.5 3.4 %all-to-all-start.7 = ((bf16[8,32,640]{2,1,0:T(8,128)(2,1)}), bf16[8,32,640]{2,1,0:T(8,128)(2,1)S(1)}, u32[]{:S(2)}, u32[]{:S(2)}) async-start(bf16[8,32,640]{2,1,0:T(8,128)(2,1)} %copy.31), calls=%async_computation.7 | async-start | bytes 655360 | tf_op jit(solution)/shard_map/all_to_all | solution.py:207
  163.9 0.1 copy.29
  164.0 6.2 %all-to-all-done.7 = bf16[8,32,640]{2,1,0:T(8,128)(2,1)S(1)} async-done(((bf16[8,32,640]{2,1,0:T(8,128)(2,1)}), bf16[8,32,640]{2,1,0:T(8,128)(2,1)S(1)}, u32[]{:S(2)}, u32[]{:S(2)}) %all-to-all-start.7) | async-done | bytes 327712 | tf_op jit(solution)/shard_map/all_to_all | solution.py:207
  170.2 0.2 copy.32
  170.5 0.5 copy.33
  170.9 1.2 reshape.96
  (5 shorter events, 0.1 us)
Async XLA Ops:
  25.5 7.7 %slice-start.1 = ((bf16[256,1152]{1,0:T(8,128)(2,1)}), bf16[256,640]{1,0:T(8,128)(2,1)S(1)}, s32[]{:S(2)}) async-start(bf16[256,1152]{1,0:T(8,128)(2,1)} %shard_map.46), calls=%async_computation.9 | async-start | bytes 655360 | tf_op jit(solution)/shard_map/slice | solution.py:203
  27.2 12.0 %all-to-all-start = ((bf16[8,32,512]{2,1,0:T(8,128)(2,1)}), bf16[8,32,512]{2,1,0:T(8,128)(2,1)S(1)}, u32[]{:S(2)}, u32[]{:S(2)}) async-start(bf16[8,32,512]{2,1,0:T(8,128)(2,1)} %bitcast.8), calls=%async_computation | async-start | bytes 524288 | tf_op jit(solution)/shard_map/all_to_all | solution.py:204
  39.2 27.4 %all-to-all-start.2 = ((bf16[8,32,640]{2,0,1:T(8,128)(2,1)}), bf16[8,32,640]{2,0,1:T(8,128)(2,1)S(1)}, u32[]{:S(2)}, u32[]{:S(2)}) async-start(bf16[8,32,640]{2,0,1:T(8,128)(2,1)} %copy.26), calls=%async_computation.2 | async-start | bytes 655360 | tf_op jit(solution)/shard_map/all_to_all | solution.py:205
  52.1 36.9 %copy-start = (bf16[2,2,2,20736]{3,2,1,0:T(2,128)(2,1)S(1)}, bf16[2,2,2,20736]{3,2,1,0:T(2,128)(2,1)}, u32[]{:S(2)}) copy-start(bf16[2,2,2,20736]{3,2,1,0:T(2,128)(2,1)} %param.7) | copy-start | bytes 995332
  66.6 18.8 %all-to-all-start.1 = ((bf16[8,32,512]{2,0,1:T(8,128)(2,1)}), bf16[8,32,512]{2,0,1:T(8,128)(2,1)S(1)}, u32[]{:S(2)}, u32[]{:S(2)}) async-start(bf16[8,32,512]{2,0,1:T(8,128)(2,1)} %copy.24), calls=%async_computation.1 | async-start | bytes 524288 | tf_op jit(solution)/shard_map/all_to_all | solution.py:206
  85.5 9.7 %all-to-all-start.3 = ((bf16[8,32,640]{2,1,0:T(8,128)(2,1)}), bf16[8,32,640]{2,1,0:T(8,128)(2,1)S(1)}, u32[]{:S(2)}, u32[]{:S(2)}) async-start(bf16[8,32,640]{2,1,0:T(8,128)(2,1)} %copy.27), calls=%async_computation.3 | async-start | bytes 655360 | tf_op jit(solution)/shard_map/all_to_all | solution.py:207
  108.6 5.1 %slice-start = ((bf16[256,1152]{1,0:T(8,128)(2,1)}), bf16[256,640]{1,0:T(8,128)(2,1)S(1)}, s32[]{:S(2)}) async-start(bf16[256,1152]{1,0:T(8,128)(2,1)} %shard_map.47), calls=%async_computation.8 | async-start | bytes 655360 | tf_op jit(solution)/shard_map/slice | solution.py:203
  110.3 9.4 %all-to-all-start.4 = ((bf16[8,32,512]{2,1,0:T(8,128)(2,1)}), bf16[8,32,512]{2,1,0:T(8,128)(2,1)S(1)}, u32[]{:S(2)}, u32[]{:S(2)}) async-start(bf16[8,32,512]{2,1,0:T(8,128)(2,1)} %bitcast.16), calls=%async_computation.4 | async-start | bytes 524288 | tf_op jit(solution)/shard_map/all_to_all | solution.py:204
  119.8 22.1 %all-to-all-start.6 = ((bf16[8,32,640]{2,0,1:T(8,128)(2,1)}), bf16[8,32,640]{2,0,1:T(8,128)(2,1)S(1)}, u32[]{:S(2)}, u32[]{:S(2)}) async-start(bf16[8,32,640]{2,0,1:T(8,128)(2,1)} %copy.30), calls=%async_computation.6 | async-start | bytes 655360 | tf_op jit(solution)/shard_map/all_to_all | solution.py:205
  141.8 18.6 %all-to-all-start.5 = ((bf16[8,32,512]{2,0,1:T(8,128)(2,1)}), bf16[8,32,512]{2,0,1:T(8,128)(2,1)S(1)}, u32[]{:S(2)}, u32[]{:S(2)}) async-start(bf16[8,32,512]{2,0,1:T(8,128)(2,1)} %copy.28), calls=%async_computation.5 | async-start | bytes 524288 | tf_op jit(solution)/shard_map/all_to_all | solution.py:206
  160.5 9.7 %all-to-all-start.7 = ((bf16[8,32,640]{2,1,0:T(8,128)(2,1)}), bf16[8,32,640]{2,1,0:T(8,128)(2,1)S(1)}, u32[]{:S(2)}, u32[]{:S(2)}) async-start(bf16[8,32,640]{2,1,0:T(8,128)(2,1)} %copy.31), calls=%async_computation.7 | async-start | bytes 655360 | tf_op jit(solution)/shard_map/all_to_all | solution.py:207

commit v3 on v1

--- a/solution.py
+++ b/solution.py
@@ -96,11 +96,15 @@
     rows = s0.shape[1]
     block = rows // 4
     if packed_in:
-        whole = x_ref[...].astype(jnp.float32)
         lane = lax.broadcasted_iota(jnp.int32, (block, WIDE), 1)
+        parts = []
+        for r in range(2):
+            v = x_ref[:, r, :].astype(jnp.float32)
+            parts.append(jnp.concatenate([v, jnp.zeros((block, 640 - 4 * P_SIZE), jnp.float32)], 1))
         for b in range(4):
-            piece = whole if b == 0 else pltpu.roll(whole, 4 * F - b * F, 1)
-            piece = jnp.where(lane < F, piece[:, :WIDE], 0.0)
+            re = pltpu.roll(parts[0], (640 - b * P_SIZE) % 640, 1)[:, :WIDE]
+            im = pltpu.roll(parts[1], (640 + P_SIZE - b * P_SIZE) % 640, 1)[:, :WIDE]
+            piece = jnp.where(lane < P_SIZE, re, jnp.where(lane < F, im, 0.0))
             for q in range(WIDE // 128):
                 s0[q, b * block:(b + 1) * block, :] = piece[:, q * 128:(q + 1) * 128]
     else:
@@ -126,15 +130,21 @@
             out = (y * cs + swapped * sn).astype(jnp.bfloat16).astype(jnp.float32)
             store_class(dst, fixed, out)
     last = bufs[len(levels) % 2]
-    total = None
-    pad = jnp.zeros((block, 4 * F - WIDE), jnp.float32)
+    lane = lax.broadcasted_iota(jnp.int32, (block, 640), 1)
+    pad = jnp.zeros((block, 640 - WIDE), jnp.float32)
+    totals = [None, None]
     for b in range(4):
         piece = jnp.concatenate([last[q, b * block:(b + 1) * block, :] for q in range(WIDE // 128)], 1)
         piece = jnp.concatenate([piece, pad], 1)
+        re = jnp.where(lane < P_SIZE, piece, 0.0)
+        im = jnp.where((lane >= P_SIZE) & (lane < F), piece, 0.0)
         if b:
-            piece = pltpu.roll(piece, b * F, 1)
-        total = piece if total is None else total + piece
-    o_ref[...] = total.astype(o_ref.dtype)
+            re = pltpu.roll(re, b * P_SIZE, 1)
+        im = pltpu.roll(im, (640 + b * P_SIZE - P_SIZE) % 640, 1)
+        totals[0] = re if totals[0] is None else totals[0] + re
+        totals[1] = im if totals[1] is None else totals[1] + im
+    for r in range(2):
+        o_ref[:, r, :] = totals[r][:, :4 * P_SIZE].astype(o_ref.dtype)
 
 
 def run_levels(levels, packed_in, x, f_t, m_list):
@@ -146,7 +156,7 @@
     m_list = [jnp.pad(m, [(0, 0)] * 4 + [(0, LANE - P_SIZE)]) for m in m_list]
     return pl.pallas_call(
         functools.partial(levels_kernel, levels, packed_in),
-        out_shape=jax.ShapeDtypeStruct((rows // 4, 4 * F), jnp.bfloat16),
+        out_shape=jax.ShapeDtypeStruct((rows // 4, 2, 4 * P_SIZE), jnp.bfloat16),
         in_specs=[vmem] * (2 + len(m_list)),
         out_specs=vmem,
         scratch_shapes=[pltpu.VMEM((WIDE // 128, rows, 128), jnp.float32)] * 4 + w_scratch,
@@ -215,7 +225,7 @@
     levels2 = [("quad", (5, 0)), ("quad", (6, 1)), ("quad", (7, 2)), ("pair", (3,)), ("pair", (4,))]
     y2 = run_levels(levels2, True, z, f2, [wq, wp])
     w = lax.all_to_all(y2, ("gx", "gy"), 0, 0, tiled=True)
-    w = w.reshape(256, 4, F).transpose(2, 1, 0)
+    w = w.reshape(256, 2, 4, P_SIZE).transpose(1, 3, 2, 0)
     return w.reshape(F, 1, 1, 1024)
 
 

time: 119 us -> 112 us (0.941)
  local copies, waits for them, and re-layouts: 21 us -> 15.9 us
  other arithmetic: 6.33 us -> 2.39 us
  Pallas kernels: 26 us -> 27.5 us
    unnamed x8 -> x5, local copies, waits for them, and re-layouts: 6.4 us -> 2.26 us
    all_to_all x2 -> x0, other arithmetic: 3.96 us -> none  [the longest x1 1.98 us: local(): z = lax.all_to_all(y1, ('gx', 'gy'), 0, 0, tiled=True)]
    pallas_call x2, Pallas kernels: 26 us -> 27.5 us  [run_levels(): pl.pallas_call(functools.partial(levels_kernel, levels, packed_in), out_s...]
  transfers between devices with their start and end apart: 1 -> 1, of which waited for: 1 -> 1; matrix products, arithmetic and copies ran while one was open for 2% -> 3% of each run, Pallas kernels for 0% -> 0%
where the time goes in v3:
time: 112 us
  blocking collectives  30.7 us (27%)
  Pallas kernels  27.5 us (25%)
  waiting for transfers between devices  19.9 us (18%)
  local copies, waits for them, and re-layouts  15.9 us (14%)
  starting transfers between devices  15.6 us (14%)
  other arithmetic  2.39 us (2%)
    all_to_all x1, blocking collectives, local(): w = lax.all_to_all(y2, ('gx', 'gy'), 0, 0, tiled=True)  30.7 us
    pallas_call x2, Pallas kernels, run_levels(): pl.pallas_call(functools.partial(levels_kernel, levels, packed_in), out_s...  27.5 us
    all_to_all x1, waiting for transfers between devices, local(): z = lax.all_to_all(y1, ('gx', 'gy'), 0, 0, tiled=True)  19.9 us
    all_to_all x1, starting transfers between devices, local(): z = lax.all_to_all(y1, ('gx', 'gy'), 0, 0, tiled=True)  15.6 us
    reshape x1, local copies, waits for them, and re-layouts, local(): wq = quad.reshape(4, 4, 2, P_SIZE, P_SIZE)  5.48 us
    pad x2, local copies, waits for them, and re-layouts, run_levels(): m_list = [jnp.pad(m, [(0, 0)] * 4 + [(0, LANE - P_SIZE)]) for m in m_list]  2.75 us
    unnamed x5, local copies, waits for them, and re-layouts  2.26 us
  transfers between devices with their start and end apart: 1, of which 1 were waited for; matrix products, arithmetic and copies ran while one was open for 3% of the time, Pallas kernels for 0%

profile of v3, /device:TPU:1, one launch (start us, length us, event | category | flops | bytes accessed | tf_op | source)
XLA Modules:
  0.0 112.1 jit_solution(660522005385048701)
XLA Ops:
  0.0 0.8 fusion.8
  0.8 5.5 %reshape.61 = bf16[4,4,2,144,144]{4,3,2,1,0:T(8,128)(2,1)S(1)} reshape(bf16[4,4,2,20736]{3,2,1,0:T(2,128)(2,1)} %param.6) | data formatting | bytes 2654208 | tf_op jit(solution)/shard_map/reshape | solution.py:212
  6.3 1.4 %copy.9 = bf16[288,1,1,1024]{0,3,2,1:T(8,128)(2,1)S(1)} copy(bf16[288,1,1,1024]{3,0,2,1:T(8,128)(2,1)} %param.4) | data formatting | bytes 1179648 | tf_op args[0]
  7.7 1.8 %pad.43.refs_0_ = bf16[4,4,2,144,256]{4,3,2,1,0:T(8,128)(2,1)} pad(bf16[4,4,2,144,144]{4,3,2,1,0:T(8,128)(2,1)S(1)} %reshape.61, bf16[]{:T(256)} %constant.13.clone.1), padding=0_0x0_0x0_0x0_0x0_112 | pad | bytes 3686402 | tf_op jit(solution)/shard_map/jit(_pad)/pad | solution.py:156
  9.6 1.0 pad.38.x_ref
  10.5 0.3 multiply_cosine_fusion.1
  10.9 0.1 fusion.6
  10.9 0.3 multiply_cosine_fusion
  11.3 0.1 fusion.4
  11.4 0.7 pad_maximum_fusion.f_ref
  12.0 0.0 copy-start.1
  12.1 13.7 %shard_map.46 = bf16[256,2,576]{2,1,0:T(2,128)(2,1)} custom-call(bf16[1024,384]{1,0:T(8,128)(2,1)} %pad.38.x_ref, f32[4,32,384]{2,1,0:T(8,128)} %pad_maximum_fusion.f_ref, bf16[4,4,2,144,256]{4,3,2,1,0:T(8,128)(2,1)} %pad.43.refs_0_), custom_call_target="tpu_custom_call" | custom-call | tf_op jit(solution)/shard_map/pallas_call | solution.py:157
  25.7 15.6 %all-to-all-start = ((bf16[256,2,576]{2,1,0:T(2,128)(2,1)}), bf16[256,2,576]{2,1,0:T(2,128)(2,1)S(1)}, u32[]{:S(2)}, u32[]{:S(2)}) async-start(bf16[256,2,576]{2,1,0:T(2,128)(2,1)} %shard_map.46), calls=%async_computation | async-start | bytes 1310720 | tf_op jit(solution)/shard_map/all_to_all | solution.py:221
  41.4 0.0 copy-done.1
  41.4 1.1 reshape.62
  42.5 0.9 pad.48.refs_1_
  43.4 0.1 fusion.2
  43.5 0.1 fusion
  43.6 0.7 pad_maximum_fusion.1.f_ref
  44.3 19.9 %all-to-all-done.x_ref = bf16[256,2,576]{2,1,0:T(2,128)(2,1)S(1)} async-done(((bf16[256,2,576]{2,1,0:T(2,128)(2,1)}), bf16[256,2,576]{2,1,0:T(2,128)(2,1)S(1)}, u32[]{:S(2)}, u32[]{:S(2)}) %all-to-all-start) | async-done | bytes 589856 | tf_op jit(solution)/shard_map/all_to_all | solution.py:221
  64.2 0.0 copy-start
  64.2 0.8 copy-done
  65.0 13.8 %shard_map.47 = bf16[256,2,576]{2,1,0:T(2,128)(2,1)} custom-call(bf16[256,2,576]{2,1,0:T(2,128)(2,1)} %copy-done, f32[4,32,384]{2,1,0:T(8,128)} %pad_maximum_fusion.1.f_ref, bf16[4,4,2,144,256]{4,3,2,1,0:T(8,128)(2,1)} %pad.43.refs_0_, bf16[2,2,2,144,256]{4,3,2,1,0:T(8,128)(2,1)} %pad.48.refs_1_), custom_call_target="tpu_custom_call" | custom-call | tf_op jit(solution)/shard_map/pallas_call | solution.py:157
  78.9 30.7 %all_to_all.10 = bf16[256,2,576]{2,1,0:T(2,128)(2,1)S(1)} all-to-all(bf16[256,2,576]{2,1,0:T(2,128)(2,1)} %shard_map.47), channel_id=1, replica_groups=mesh['gx'=8,'gy'=32] {'gx','gy'}, dimensions={0} | all-to-all | bytes 1179648 | tf_op jit(solution)/shard_map/all_to_all | solution.py:227
  109.5 1.0 copy.10
  110.6 0.3 copy.11
  110.9 1.2 %reshape.64 = bf16[288,1,1,1024]{3,0,2,1:T(8,128)(2,1)} reshape(bf16[2,144,4,256]{3,2,1,0:T(4,128)(2,1)S(1)} %copy.11) | data formatting | bytes 1179648 | tf_op jit(solution)/shard_map/reshape | solution.py:229
  (4 shorter events, 0.0 us)
Async XLA Ops:
  12.0 29.4 %copy-start.1 = (bf16[2,2,2,20736]{3,2,1,0:T(2,128)(2,1)S(1)}, bf16[2,2,2,20736]{3,2,1,0:T(2,128)(2,1)}, u32[]{:S(2)}) copy-start(bf16[2,2,2,20736]{3,2,1,0:T(2,128)(2,1)} %param.7) | copy-start | bytes 995332
  25.7 38.4 %all-to-all-start = ((bf16[256,2,576]{2,1,0:T(2,128)(2,1)}), bf16[256,2,576]{2,1,0:T(2,128)(2,1)S(1)}, u32[]{:S(2)}, u32[]{:S(2)}) async-start(bf16[256,2,576]{2,1,0:T(2,128)(2,1)} %shard_map.46), calls=%async_computation | async-start | bytes 1310720 | tf_op jit(solution)/shard_map/all_to_all | solution.py:221
  64.2 0.8 copy-start

commit v4 on v3

--- a/solution.py
+++ b/solution.py
@@ -43,7 +43,7 @@
     low = min(fixed)
     base = sum(v << p for p, v in fixed.items())
     free = [p for p in range(rows.bit_length() - 1) if p not in fixed]
-    if (1 << low) >= 8:
+    if (1 << low) >= 8 and len(fixed) > 1:
         outer = [p for p in free if p > low]
         starts = []
         for k in range(1 << len(outer)):
@@ -108,8 +108,10 @@
             for q in range(WIDE // 128):
                 s0[q, b * block:(b + 1) * block, :] = piece[:, q * 128:(q + 1) * 128]
     else:
+        v = x_ref[...].astype(jnp.float32)
+        v = jnp.concatenate([v, jnp.zeros((WIDE - F, rows), jnp.float32)], 0).T
         for q in range(WIDE // 128):
-            s0[q] = x_ref[:, q * 128:(q + 1) * 128].astype(jnp.float32)
+            s0[q] = v[:, q * 128:(q + 1) * 128]
     bufs = (s0, s1)
     for index, (kind, bits) in enumerate(levels):
         src = bufs[index % 2]
@@ -214,8 +216,7 @@
     group = jnp.arange(32, dtype=jnp.int32)
 
     f1 = factors(slope, place_x * 32 + group, place_y * 32 + group)
-    x = source.reshape(F, 1024).T
-    x = jnp.pad(x, [(0, 0), (0, WIDE - F)])
+    x = source.reshape(F, 1024)
     levels1 = [("quad", (k + 5, k)) for k in range(5)]
     y1 = run_levels(levels1, False, x, f1, [wq])
     z = lax.all_to_all(y1, ("gx", "gy"), 0, 0, tiled=True)

time: 112 us -> 115 us (1.027)
  Pallas kernels: 27.5 us -> 32.6 us
  local copies, waits for them, and re-layouts: 15.9 us -> 13.5 us
    pallas_call x2, Pallas kernels: 27.5 us -> 32.6 us  [run_levels(): pl.pallas_call(functools.partial(levels_kernel, levels, packed_in), out_s...]
    unnamed x5 -> x4, local copies, waits for them, and re-layouts: 2.26 us -> 0.85 us
  transfers between devices with their start and end apart: 1 -> 1, of which waited for: 1 -> 1; matrix products, arithmetic and copies ran while one was open for 3% -> 2% of each run, Pallas kernels for 0% -> 0%
where the time goes in v4:
time: 115 us
  Pallas kernels  32.6 us (28%)
  blocking collectives  30.4 us (26%)
  waiting for transfers between devices  19.7 us (17%)
  starting transfers between devices  15.8 us (14%)
  local copies, waits for them, and re-layouts  13.5 us (12%)
  other arithmetic  2.36 us (2%)
    pallas_call x2, Pallas kernels, run_levels(): pl.pallas_call(functools.partial(levels_kernel, levels, packed_in), out_s...  32.6 us
    all_to_all x1, blocking collectives, local(): w = lax.all_to_all(y2, ('gx', 'gy'), 0, 0, tiled=True)  30.4 us
    all_to_all x1, waiting for transfers between devices, local(): z = lax.all_to_all(y1, ('gx', 'gy'), 0, 0, tiled=True)  19.7 us
    all_to_all x1, starting transfers between devices, local(): z = lax.all_to_all(y1, ('gx', 'gy'), 0, 0, tiled=True)  15.8 us
    reshape x1, local copies, waits for them, and re-layouts, local(): wq = quad.reshape(4, 4, 2, P_SIZE, P_SIZE)  5.48 us
    pad x2, local copies, waits for them, and re-layouts, run_levels(): m_list = [jnp.pad(m, [(0, 0)] * 4 + [(0, LANE - P_SIZE)]) for m in m_list]  2.75 us
  transfers between devices with their start and end apart: 1, of which 1 were waited for; matrix products, arithmetic and copies ran while one was open for 2% of the time, Pallas kernels for 0%

profile of v4, /device:TPU:1, one launch (start us, length us, event | category | flops | bytes accessed | tf_op | source)
XLA Modules:
  0.0 114.5 jit_solution(471111869798449656)
XLA Ops:
  0.0 0.8 fusion.8
  0.8 5.5 %reshape.61 = bf16[4,4,2,144,144]{4,3,2,1,0:T(8,128)(2,1)S(1)} reshape(bf16[4,4,2,20736]{3,2,1,0:T(2,128)(2,1)} %param.6) | data formatting | bytes 2654208 | tf_op jit(solution)/shard_map/reshape | solution.py:214
  6.3 0.3 multiply_cosine_fusion.1
  6.6 0.1 fusion.6
  6.7 0.3 multiply_cosine_fusion
  7.0 0.1 fusion.4
  7.1 1.8 %pad.38.refs_0_ = bf16[4,4,2,144,256]{4,3,2,1,0:T(8,128)(2,1)} pad(bf16[4,4,2,144,144]{4,3,2,1,0:T(8,128)(2,1)S(1)} %reshape.61, bf16[]{:T(256)} %constant.37.clone.1), padding=0_0x0_0x0_0x0_0x0_112 | pad | bytes 3686402 | tf_op jit(solution)/shard_map/jit(_pad)/pad | solution.py:158
  9.0 0.7 pad_maximum_fusion.f_ref
  9.6 0.0 copy-start.1
  9.6 13.8 %shard_map.46 = bf16[256,2,576]{2,1,0:T(2,128)(2,1)} custom-call(bf16[288,1024]{1,0:T(8,128)(2,1)} %bitcast.23, f32[4,32,384]{2,1,0:T(8,128)} %pad_maximum_fusion.f_ref, bf16[4,4,2,144,256]{4,3,2,1,0:T(8,128)(2,1)} %pad.38.refs_0_), custom_call_target="tpu_custom_call" | custom-call | tf_op jit(solution)/shard_map/pallas_call | solution.py:159
  23.5 15.8 %all-to-all-start = ((bf16[256,2,576]{2,1,0:T(2,128)(2,1)}), bf16[256,2,576]{2,1,0:T(2,128)(2,1)S(1)}, u32[]{:S(2)}, u32[]{:S(2)}) async-start(bf16[256,2,576]{2,1,0:T(2,128)(2,1)} %shard_map.46), calls=%async_computation | async-start | bytes 1310720 | tf_op jit(solution)/shard_map/all_to_all | solution.py:222
  39.3 0.0 copy-done.1
  39.3 1.1 reshape.62
  40.4 0.9 pad.43.refs_1_
  41.3 0.1 fusion.2
  41.4 0.1 fusion
  41.5 0.7 pad_maximum_fusion.1.f_ref
  42.2 19.7 %all-to-all-done.x_ref = bf16[256,2,576]{2,1,0:T(2,128)(2,1)S(1)} async-done(((bf16[256,2,576]{2,1,0:T(2,128)(2,1)}), bf16[256,2,576]{2,1,0:T(2,128)(2,1)S(1)}, u32[]{:S(2)}, u32[]{:S(2)}) %all-to-all-start) | async-done | bytes 589856 | tf_op jit(solution)/shard_map/all_to_all | solution.py:222
  61.9 0.0 copy-start
  61.9 0.8 copy-done
  62.8 18.7 %shard_map.47 = bf16[256,2,576]{2,1,0:T(2,128)(2,1)} custom-call(bf16[256,2,576]{2,1,0:T(2,128)(2,1)} %copy-done, f32[4,32,384]{2,1,0:T(8,128)} %pad_maximum_fusion.1.f_ref, bf16[4,4,2,144,256]{4,3,2,1,0:T(8,128)(2,1)} %pad.38.refs_0_, bf16[2,2,2,144,256]{4,3,2,1,0:T(8,128)(2,1)} %pad.43.refs_1_), custom_call_target="tpu_custom_call" | custom-call | tf_op jit(solution)/shard_map/pallas_call | solution.py:159
  81.5 30.4 %all_to_all.10 = bf16[256,2,576]{2,1,0:T(2,128)(2,1)S(1)} all-to-all(bf16[256,2,576]{2,1,0:T(2,128)(2,1)} %shard_map.47), channel_id=1, replica_groups=mesh['gx'=8,'gy'=32] {'gx','gy'}, dimensions={0} | all-to-all | bytes 1179648 | tf_op jit(solution)/shard_map/all_to_all | solution.py:228
  111.9 1.0 copy.7
  113.0 0.3 copy.8
  113.3 1.2 %reshape.64 = bf16[288,1,1,1024]{3,0,2,1:T(8,128)(2,1)} reshape(bf16[2,144,4,256]{3,2,1,0:T(4,128)(2,1)S(1)} %copy.8) | data formatting | bytes 1179648 | tf_op jit(solution)/shard_map/reshape | solution.py:230
  (4 shorter events, 0.0 us)
Async XLA Ops:
  9.6 29.7 %copy-start.1 = (bf16[2,2,2,20736]{3,2,1,0:T(2,128)(2,1)S(1)}, bf16[2,2,2,20736]{3,2,1,0:T(2,128)(2,1)}, u32[]{:S(2)}) copy-start(bf16[2,2,2,20736]{3,2,1,0:T(2,128)(2,1)} %param.7) | copy-start | bytes 995332
  23.5 38.4 %all-to-all-start = ((bf16[256,2,576]{2,1,0:T(2,128)(2,1)}), bf16[256,2,576]{2,1,0:T(2,128)(2,1)S(1)}, u32[]{:S(2)}, u32[]{:S(2)}) async-start(bf16[256,2,576]{2,1,0:T(2,128)(2,1)} %shard_map.46), calls=%async_computation | async-start | bytes 1310720 | tf_op jit(solution)/shard_map/all_to_all | solution.py:222
  61.9 0.8 copy-start

commit v5 on v4

--- a/solution.py
+++ b/solution.py
@@ -43,7 +43,7 @@
     low = min(fixed)
     base = sum(v << p for p, v in fixed.items())
     free = [p for p in range(rows.bit_length() - 1) if p not in fixed]
-    if (1 << low) >= 8 and len(fixed) > 1:
+    if (1 << low) >= 8:
         outer = [p for p in free if p > low]
         starts = []
         for k in range(1 << len(outer)):

time: 115 us -> 110 us (0.957)
  Pallas kernels: 32.6 us -> 27.7 us
    pallas_call x2, Pallas kernels: 32.6 us -> 27.7 us  [run_levels(): pl.pallas_call(functools.partial(levels_kernel, levels, packed_in), out_s...]
  transfers between devices with their start and end apart: 1 -> 1, of which waited for: 1 -> 1; matrix products, arithmetic and copies ran while one was open for 2% -> 3% of each run, Pallas kernels for 0% -> 0%
where the time goes in v5:
time: 110 us
  blocking collectives  30.6 us (28%)
  Pallas kernels  27.7 us (25%)
  waiting for transfers between devices  19.9 us (18%)
  starting transfers between devices  15.7 us (14%)
  local copies, waits for them, and re-layouts  13.5 us (12%)
  other arithmetic  2.36 us (2%)
    all_to_all x1, blocking collectives, local(): w = lax.all_to_all(y2, ('gx', 'gy'), 0, 0, tiled=True)  30.6 us
    pallas_call x2, Pallas kernels, run_levels(): pl.pallas_call(functools.partial(levels_kernel, levels, packed_in), out_s...  27.7 us
    all_to_all x1, waiting for transfers between devices, local(): z = lax.all_to_all(y1, ('gx', 'gy'), 0, 0, tiled=True)  19.9 us
    all_to_all x1, starting transfers between devices, local(): z = lax.all_to_all(y1, ('gx', 'gy'), 0, 0, tiled=True)  15.7 us
    reshape x1, local copies, waits for them, and re-layouts, local(): wq = quad.reshape(4, 4, 2, P_SIZE, P_SIZE)  5.48 us
    pad x2, local copies, waits for them, and re-layouts, run_levels(): m_list = [jnp.pad(m, [(0, 0)] * 4 + [(0, LANE - P_SIZE)]) for m in m_list]  2.75 us
  transfers between devices with their start and end apart: 1, of which 1 were waited for; matrix products, arithmetic and copies ran while one was open for 3% of the time, Pallas kernels for 0%

profile of v5, /device:TPU:1, one launch (start us, length us, event | category | flops | bytes accessed | tf_op | source)
XLA Modules:
  0.0 109.9 jit_solution(431424922048725805)
XLA Ops:
  0.0 0.8 fusion.8
  0.8 5.5 %reshape.61 = bf16[4,4,2,144,144]{4,3,2,1,0:T(8,128)(2,1)S(1)} reshape(bf16[4,4,2,20736]{3,2,1,0:T(2,128)(2,1)} %param.6) | data formatting | bytes 2654208 | tf_op jit(solution)/shard_map/reshape | solution.py:214
  6.3 0.3 multiply_cosine_fusion.1
  6.6 0.1 fusion.6
  6.7 0.3 multiply_cosine_fusion
  7.0 0.1 fusion.4
  7.1 1.8 %pad.38.refs_0_ = bf16[4,4,2,144,256]{4,3,2,1,0:T(8,128)(2,1)} pad(bf16[4,4,2,144,144]{4,3,2,1,0:T(8,128)(2,1)S(1)} %reshape.61, bf16[]{:T(256)} %constant.37.clone.1), padding=0_0x0_0x0_0x0_0x0_112 | pad | bytes 3686402 | tf_op jit(solution)/shard_map/jit(_pad)/pad | solution.py:158
  9.0 0.7 pad_maximum_fusion.f_ref
  9.6 0.0 copy-start.1
  9.6 13.8 %shard_map.46 = bf16[256,2,576]{2,1,0:T(2,128)(2,1)} custom-call(bf16[288,1024]{1,0:T(8,128)(2,1)} %bitcast.23, f32[4,32,384]{2,1,0:T(8,128)} %pad_maximum_fusion.f_ref, bf16[4,4,2,144,256]{4,3,2,1,0:T(8,128)(2,1)} %pad.38.refs_0_), custom_call_target="tpu_custom_call" | custom-call | tf_op jit(solution)/shard_map/pallas_call | solution.py:159
  23.5 15.7 %all-to-all-start = ((bf16[256,2,576]{2,1,0:T(2,128)(2,1)}), bf16[256,2,576]{2,1,0:T(2,128)(2,1)S(1)}, u32[]{:S(2)}, u32[]{:S(2)}) async-start(bf16[256,2,576]{2,1,0:T(2,128)(2,1)} %shard_map.46), calls=%async_computation | async-start | bytes 1310720 | tf_op jit(solution)/shard_map/all_to_all | solution.py:222
  39.1 0.0 copy-done.1
  39.2 1.1 reshape.62
  40.2 0.9 pad.43.refs_1_
  41.2 0.1 fusion.2
  41.2 0.1 fusion
  41.3 0.7 pad_maximum_fusion.1.f_ref
  42.0 19.9 %all-to-all-done.x_ref = bf16[256,2,576]{2,1,0:T(2,128)(2,1)S(1)} async-done(((bf16[256,2,576]{2,1,0:T(2,128)(2,1)}), bf16[256,2,576]{2,1,0:T(2,128)(2,1)S(1)}, u32[]{:S(2)}, u32[]{:S(2)}) %all-to-all-start) | async-done | bytes 589856 | tf_op jit(solution)/shard_map/all_to_all | solution.py:222
  61.9 0.0 copy-start
  61.9 0.8 copy-done
  62.8 13.9 %shard_map.47 = bf16[256,2,576]{2,1,0:T(2,128)(2,1)} custom-call(bf16[256,2,576]{2,1,0:T(2,128)(2,1)} %copy-done, f32[4,32,384]{2,1,0:T(8,128)} %pad_maximum_fusion.1.f_ref, bf16[4,4,2,144,256]{4,3,2,1,0:T(8,128)(2,1)} %pad.38.refs_0_, bf16[2,2,2,144,256]{4,3,2,1,0:T(8,128)(2,1)} %pad.43.refs_1_), custom_call_target="tpu_custom_call" | custom-call | tf_op jit(solution)/shard_map/pallas_call | solution.py:159
  76.6 30.6 %all_to_all.10 = bf16[256,2,576]{2,1,0:T(2,128)(2,1)S(1)} all-to-all(bf16[256,2,576]{2,1,0:T(2,128)(2,1)} %shard_map.47), channel_id=1, replica_groups=mesh['gx'=8,'gy'=32] {'gx','gy'}, dimensions={0} | all-to-all | bytes 1179648 | tf_op jit(solution)/shard_map/all_to_all | solution.py:228
  107.3 1.0 copy.7
  108.3 0.3 copy.8
  108.6 1.2 %reshape.64 = bf16[288,1,1,1024]{3,0,2,1:T(8,128)(2,1)} reshape(bf16[2,144,4,256]{3,2,1,0:T(4,128)(2,1)S(1)} %copy.8) | data formatting | bytes 1179648 | tf_op jit(solution)/shard_map/reshape | solution.py:230
  (4 shorter events, 0.0 us)
Async XLA Ops:
  9.6 29.5 %copy-start.1 = (bf16[2,2,2,20736]{3,2,1,0:T(2,128)(2,1)S(1)}, bf16[2,2,2,20736]{3,2,1,0:T(2,128)(2,1)}, u32[]{:S(2)}) copy-start(bf16[2,2,2,20736]{3,2,1,0:T(2,128)(2,1)} %param.7) | copy-start | bytes 995332
  23.5 38.4 %all-to-all-start = ((bf16[256,2,576]{2,1,0:T(2,128)(2,1)}), bf16[256,2,576]{2,1,0:T(2,128)(2,1)S(1)}, u32[]{:S(2)}, u32[]{:S(2)}) async-start(bf16[256,2,576]{2,1,0:T(2,128)(2,1)} %shard_map.46), calls=%async_computation | async-start | bytes 1310720 | tf_op jit(solution)/shard_map/all_to_all | solution.py:222
  61.9 0.8 copy-start

commit v6 on v5

--- a/solution.py
+++ b/solution.py
@@ -211,7 +211,7 @@
 def local(source, slope, quad, pair):
     place_x = lax.axis_index("gx")
     place_y = lax.axis_index("gy")
-    wq = quad.reshape(4, 4, 2, P_SIZE, P_SIZE)
+    wq = lax.optimization_barrier(quad.astype(jnp.float32)).reshape(4, 4, 2, P_SIZE, P_SIZE)
     wp = pair.reshape(2, 2, 2, P_SIZE, P_SIZE)
     group = jnp.arange(32, dtype=jnp.int32)
 

time: 110 us -> 118 us (1.073)
  local copies, waits for them, and re-layouts: 13.5 us -> 17.5 us
  other arithmetic: 2.36 us -> 4.59 us
  Pallas kernels: 27.7 us -> 29.1 us
    pad x2, local copies, waits for them, and re-layouts: 2.75 us -> 5.88 us  [run_levels(): m_list = [jnp.pad(m, [(0, 0)] * 4 + [(0, LANE - P_SIZE)]) for m in m_list]]
    convert_element_type x0 -> x1, other arithmetic: none -> 2.24 us  [local(): quad.astype(jnp.float32)]
    pallas_call x2, Pallas kernels: 27.7 us -> 29.1 us  [run_levels(): pl.pallas_call(functools.partial(levels_kernel, levels, packed_in), out_s...]
  transfers between devices with their start and end apart: 1 -> 1, of which waited for: 1 -> 1; matrix products, arithmetic and copies ran while one was open for 3% -> 2% of each run, Pallas kernels for 0% -> 0%
where the time goes in v6:
time: 118 us
  blocking collectives  30.7 us (26%)
  Pallas kernels  29.1 us (25%)
  waiting for transfers between devices  19.9 us (17%)
  local copies, waits for them, and re-layouts  17.5 us (15%)
  starting transfers between devices  15.7 us (13%)
  other arithmetic  4.59 us (4%)
    all_to_all x1, blocking collectives, local(): w = lax.all_to_all(y2, ('gx', 'gy'), 0, 0, tiled=True)  30.7 us
    pallas_call x2, Pallas kernels, run_levels(): pl.pallas_call(functools.partial(levels_kernel, levels, packed_in), out_s...  29.1 us
    all_to_all x1, waiting for transfers between devices, local(): z = lax.all_to_all(y1, ('gx', 'gy'), 0, 0, tiled=True)  19.9 us
    all_to_all x1, starting transfers between devices, local(): z = lax.all_to_all(y1, ('gx', 'gy'), 0, 0, tiled=True)  15.7 us
    reshape x1, local copies, waits for them, and re-layouts, local(): lax.optimization_barrier(quad.astype(jnp.float32))  6.38 us
    pad x2, local copies, waits for them, and re-layouts, run_levels(): m_list = [jnp.pad(m, [(0, 0)] * 4 + [(0, LANE - P_SIZE)]) for m in m_list]  5.88 us
  transfers between devices with their start and end apart: 1, of which 1 were waited for; matrix products, arithmetic and copies ran while one was open for 2% of the time, Pallas kernels for 0%

profile of v6, /device:TPU:1, one launch (start us, length us, event | category | flops | bytes accessed | tf_op | source)
XLA Modules:
  0.0 117.6 jit_solution(15118818038197136969)
XLA Ops:
  0.0 0.8 fusion.8
  0.8 2.2 %convert_element_type.47 = f32[4,4,2,20736]{3,2,1,0:T(2,128)S(1)} convert(bf16[4,4,2,20736]{3,2,1,0:T(2,128)(2,1)} %param.6) | non-fusion elementwise | flops 663552 | bytes 3981312 | tf_op jit(solution)/shard_map/convert_element_type | solution.py:214
  3.1 6.4 %reshape.61 = f32[4,4,2,144,144]{4,3,2,1,0:T(8,128)} reshape(f32[4,4,2,20736]{3,2,1,0:T(2,128)S(1)} %convert_element_type.47) | data formatting | bytes 5308416 | tf_op jit(solution)/shard_map/reshape | solution.py:214
  9.4 0.3 multiply_cosine_fusion.1
  9.7 0.1 fusion.6
  9.8 0.3 multiply_cosine_fusion
  10.2 0.1 fusion.4
  10.2 5.0 %pad.38.refs_0_ = f32[4,4,2,144,256]{4,3,2,1,0:T(8,128)} pad(f32[4,4,2,144,144]{4,3,2,1,0:T(8,128)} %reshape.61, f32[]{:T(128)} %constant.34.clone.1), padding=0_0x0_0x0_0x0_0x0_112 | pad | bytes 7372804 | tf_op jit(solution)/shard_map/jit(_pad)/pad | solution.py:158
  15.2 0.0 copy-start.1
  15.2 0.7 pad_maximum_fusion.f_ref
  15.9 14.5 %shard_map.46 = bf16[256,2,576]{2,1,0:T(2,128)(2,1)} custom-call(bf16[288,1024]{1,0:T(8,128)(2,1)} %bitcast.23, f32[4,32,384]{2,1,0:T(8,128)} %pad_maximum_fusion.f_ref, f32[4,4,2,144,256]{4,3,2,1,0:T(8,128)} %pad.38.refs_0_), custom_call_target="tpu_custom_call" | custom-call | tf_op jit(solution)/shard_map/pallas_call | solution.py:159
  30.4 15.7 %all-to-all-start = ((bf16[256,2,576]{2,1,0:T(2,128)(2,1)}), bf16[256,2,576]{2,1,0:T(2,128)(2,1)S(1)}, u32[]{:S(2)}, u32[]{:S(2)}) async-start(bf16[256,2,576]{2,1,0:T(2,128)(2,1)} %shard_map.46), calls=%async_computation | async-start | bytes 1310720 | tf_op jit(solution)/shard_map/all_to_all | solution.py:222
  46.1 0.0 copy-done.1
  46.1 1.1 reshape.62
  47.2 0.9 pad.43.refs_1_
  48.1 0.1 fusion.2
  48.2 0.1 fusion
  48.3 0.7 pad_maximum_fusion.1.f_ref
  49.0 19.9 %all-to-all-done.x_ref = bf16[256,2,576]{2,1,0:T(2,128)(2,1)S(1)} async-done(((bf16[256,2,576]{2,1,0:T(2,128)(2,1)}), bf16[256,2,576]{2,1,0:T(2,128)(2,1)S(1)}, u32[]{:S(2)}, u32[]{:S(2)}) %all-to-all-start) | async-done | bytes 589856 | tf_op jit(solution)/shard_map/all_to_all | solution.py:222
  68.9 0.0 copy-start
  68.9 0.8 copy-done
  69.7 14.6 %shard_map.47 = bf16[256,2,576]{2,1,0:T(2,128)(2,1)} custom-call(bf16[256,2,576]{2,1,0:T(2,128)(2,1)} %copy-done, f32[4,32,384]{2,1,0:T(8,128)} %pad_maximum_fusion.1.f_ref, f32[4,4,2,144,256]{4,3,2,1,0:T(8,128)} %pad.38.refs_0_, bf16[2,2,2,144,256]{4,3,2,1,0:T(8,128)(2,1)} %pad.43.refs_1_), custom_call_target="tpu_custom_call" | custom-call | tf_op jit(solution)/shard_map/pallas_call | solution.py:159
  84.3 30.7 %all_to_all.10 = bf16[256,2,576]{2,1,0:T(2,128)(2,1)S(1)} all-to-all(bf16[256,2,576]{2,1,0:T(2,128)(2,1)} %shard_map.47), channel_id=1, replica_groups=mesh['gx'=8,'gy'=32] {'gx','gy'}, dimensions={0} | all-to-all | bytes 1179648 | tf_op jit(solution)/shard_map/all_to_all | solution.py:228
  115.0 1.0 copy.7
  116.0 0.3 copy.8
  116.3 1.2 %reshape.64 = bf16[288,1,1,1024]{3,0,2,1:T(8,128)(2,1)} reshape(bf16[2,144,4,256]{3,2,1,0:T(4,128)(2,1)S(1)} %copy.8) | data formatting | bytes 1179648 | tf_op jit(solution)/shard_map/reshape | solution.py:230
  (4 shorter events, 0.0 us)
Async XLA Ops:
  15.2 30.9 %copy-start.1 = (bf16[2,2,2,20736]{3,2,1,0:T(2,128)(2,1)S(1)}, bf16[2,2,2,20736]{3,2,1,0:T(2,128)(2,1)}, u32[]{:S(2)}) copy-start(bf16[2,2,2,20736]{3,2,1,0:T(2,128)(2,1)} %param.7) | copy-start | bytes 995332
  30.4 38.4 %all-to-all-start = ((bf16[256,2,576]{2,1,0:T(2,128)(2,1)}), bf16[256,2,576]{2,1,0:T(2,128)(2,1)S(1)}, u32[]{:S(2)}, u32[]{:S(2)}) async-start(bf16[256,2,576]{2,1,0:T(2,128)(2,1)} %shard_map.46), calls=%async_computation | async-start | bytes 1310720 | tf_op jit(solution)/shard_map/all_to_all | solution.py:222
  68.9 0.8 copy-start

commit v7 on v5

--- a/solution.py
+++ b/solution.py
@@ -22,18 +22,21 @@
 
 def build_weights(wt_ref, m_ref):
     count = wt_ref.shape[0]
-    zeros = jnp.zeros((P_SIZE, 128), jnp.float32)
-
-    def ext(v):
-        return jnp.concatenate([v, zeros], 1)
+    row = lax.broadcasted_iota(jnp.int32, (P_SIZE, WIDE), 0)
+    col = lax.broadcasted_iota(jnp.int32, (P_SIZE, WIDE), 1)
+    first = (col == row).astype(jnp.bfloat16)
+    second = (col == row + P_SIZE).astype(jnp.bfloat16)
+
+    def place(v, sel):
+        return jnp.dot(v, sel, preferred_element_type=jnp.float32)
 
     for t in range(count):
         wt_ref[t, F:WIDE, :] = jnp.zeros((WIDE - F, wt_ref.shape[2]), wt_ref.dtype)
         for c in range(count):
-            real = ext(m_ref[t, c, 0].astype(jnp.float32))
-            imag = ext(m_ref[t, c, 1].astype(jnp.float32))
-            top = real + pltpu.roll(-imag, P_SIZE, 1)
-            bottom = imag + pltpu.roll(real, P_SIZE, 1)
+            real = m_ref[t, c, 0]
+            imag = m_ref[t, c, 1]
+            top = place(real, first) - place(imag, second)
+            bottom = place(imag, first) + place(real, second)
             base = c * WIDE
             wt_ref[t, 0:P_SIZE, base:base + WIDE] = top.astype(wt_ref.dtype)
             wt_ref[t, P_SIZE:F, base:base + WIDE] = bottom.astype(wt_ref.dtype)
@@ -155,7 +158,6 @@
     w_scratch = [
         pltpu.VMEM((m.shape[0], WIDE, m.shape[1] * WIDE), jnp.bfloat16) for m in m_list
     ]
-    m_list = [jnp.pad(m, [(0, 0)] * 4 + [(0, LANE - P_SIZE)]) for m in m_list]
     return pl.pallas_call(
         functools.partial(levels_kernel, levels, packed_in),
         out_shape=jax.ShapeDtypeStruct((rows // 4, 2, 4 * P_SIZE), jnp.bfloat16),

time: 110 us -> 113 us (1.027)
  Pallas kernels: 27.7 us -> 32 us
  local copies, waits for them, and re-layouts: 13.5 us -> 12.2 us
    pallas_call x2, Pallas kernels: 27.7 us -> 32 us  [run_levels(): pl.pallas_call(functools.partial(levels_kernel, levels, packed_in), out_s...]
    pad x2 -> x0, local copies, waits for them, and re-layouts: 2.75 us -> none  [run_levels(): m_list = [jnp.pad(m, [(0, 0)] * 4 + [(0, LANE - P_SIZE)]) for m in m_list]]
  transfers between devices with their start and end apart: 1 -> 1, of which waited for: 1 -> 1; matrix products, arithmetic and copies ran while one was open for 3% -> 2% of each run, Pallas kernels for 0% -> 0%
where the time goes in v7:
time: 113 us
  Pallas kernels  32 us (28%)
  blocking collectives  30.4 us (27%)
  waiting for transfers between devices  20 us (18%)
  starting transfers between devices  15.6 us (14%)
  local copies, waits for them, and re-layouts  12.2 us (11%)
  other arithmetic  2.36 us (2%)
    pallas_call x2, Pallas kernels, run_levels(): pl.pallas_call(functools.partial(levels_kernel, levels, packed_in), out_s...  32 us
    all_to_all x1, blocking collectives, local(): w = lax.all_to_all(y2, ('gx', 'gy'), 0, 0, tiled=True)  30.4 us
    all_to_all x1, waiting for transfers between devices, local(): z = lax.all_to_all(y1, ('gx', 'gy'), 0, 0, tiled=True)  20 us
    all_to_all x1, starting transfers between devices, local(): z = lax.all_to_all(y1, ('gx', 'gy'), 0, 0, tiled=True)  15.6 us
    reshape x1, local copies, waits for them, and re-layouts, local(): wq = quad.reshape(4, 4, 2, P_SIZE, P_SIZE)  6.15 us
  transfers between devices with their start and end apart: 1, of which 1 were waited for; matrix products, arithmetic and copies ran while one was open for 2% of the time, Pallas kernels for 0%

profile of v7, /device:TPU:1, one launch (start us, length us, event | category | flops | bytes accessed | tf_op | source)
XLA Modules:
  0.0 112.7 jit_solution(4548193580732873698)
XLA Ops:
  0.0 0.8 fusion.8
  0.8 6.2 %reshape.61.refs_0_ = bf16[4,4,2,144,144]{4,3,2,1,0:T(8,128)(2,1)} reshape(bf16[4,4,2,20736]{3,2,1,0:T(2,128)(2,1)} %param.6) | data formatting | bytes 2654208 | tf_op jit(solution)/shard_map/reshape | solution.py:216
  7.0 0.3 multiply_cosine_fusion.1
  7.3 0.1 fusion.6
  7.4 0.3 multiply_cosine_fusion
  7.7 0.1 fusion.4
  7.8 0.7 pad_maximum_fusion.f_ref
  8.5 0.0 copy-start.1
  8.5 15.8 %shard_map.46 = bf16[256,2,576]{2,1,0:T(2,128)(2,1)} custom-call(bf16[288,1024]{1,0:T(8,128)(2,1)} %bitcast.23, f32[4,32,384]{2,1,0:T(8,128)} %pad_maximum_fusion.f_ref, bf16[4,4,2,144,144]{4,3,2,1,0:T(8,128)(2,1)} %reshape.61.refs_0_), custom_call_target="tpu_custom_call" | custom-call | tf_op jit(solution)/shard_map/pallas_call | solution.py:161
  24.3 15.6 %all-to-all-start = ((bf16[256,2,576]{2,1,0:T(2,128)(2,1)}), bf16[256,2,576]{2,1,0:T(2,128)(2,1)S(1)}, u32[]{:S(2)}, u32[]{:S(2)}) async-start(bf16[256,2,576]{2,1,0:T(2,128)(2,1)} %shard_map.46), calls=%async_computation | async-start | bytes 1310720 | tf_op jit(solution)/shard_map/all_to_all | solution.py:224
  39.9 0.0 copy-done.1
  39.9 1.9 %reshape.62.refs_1_ = bf16[2,2,2,144,144]{4,3,2,1,0:T(8,128)(2,1)} reshape(bf16[2,2,2,20736]{3,2,1,0:T(2,128)(2,1)S(1)} %copy-done.1) | data formatting | bytes 663552 | tf_op jit(solution)/shard_map/reshape | solution.py:217
  41.8 0.1 fusion.2
  41.9 0.1 fusion
  42.0 0.7 pad_maximum_fusion.1.f_ref
  42.7 20.0 %all-to-all-done.x_ref = bf16[256,2,576]{2,1,0:T(2,128)(2,1)S(1)} async-done(((bf16[256,2,576]{2,1,0:T(2,128)(2,1)}), bf16[256,2,576]{2,1,0:T(2,128)(2,1)S(1)}, u32[]{:S(2)}, u32[]{:S(2)}) %all-to-all-start) | async-done | bytes 589856 | tf_op jit(solution)/shard_map/all_to_all | solution.py:224
  62.7 0.0 copy-start
  62.7 0.8 copy-done
  63.6 16.2 %shard_map.47 = bf16[256,2,576]{2,1,0:T(2,128)(2,1)} custom-call(bf16[256,2,576]{2,1,0:T(2,128)(2,1)} %copy-done, f32[4,32,384]{2,1,0:T(8,128)} %pad_maximum_fusion.1.f_ref, bf16[4,4,2,144,144]{4,3,2,1,0:T(8,128)(2,1)} %reshape.61.refs_0_, bf16[2,2,2,144,144]{4,3,2,1,0:T(8,128)(2,1)} %reshape.62.refs_1_), custom_call_target="tpu_custom_call" | custom-call | tf_op jit(solution)/shard_map/pallas_call | solution.py:161
  79.7 30.4 %all_to_all.10 = bf16[256,2,576]{2,1,0:T(2,128)(2,1)S(1)} all-to-all(bf16[256,2,576]{2,1,0:T(2,128)(2,1)} %shard_map.47), channel_id=1, replica_groups=mesh['gx'=8,'gy'=32] {'gx','gy'}, dimensions={0} | all-to-all | bytes 1179648 | tf_op jit(solution)/shard_map/all_to_all | solution.py:230
  110.1 1.0 copy.7
  111.2 0.3 copy.8
  111.5 1.2 %reshape.64 = bf16[288,1,1,1024]{3,0,2,1:T(8,128)(2,1)} reshape(bf16[2,144,4,256]{3,2,1,0:T(4,128)(2,1)S(1)} %copy.8) | data formatting | bytes 1179648 | tf_op jit(solution)/shard_map/reshape | solution.py:232
  (4 shorter events, 0.0 us)
Async XLA Ops:
  8.5 31.5 %copy-start.1 = (bf16[2,2,2,20736]{3,2,1,0:T(2,128)(2,1)S(1)}, bf16[2,2,2,20736]{3,2,1,0:T(2,128)(2,1)}, u32[]{:S(2)}) copy-start(bf16[2,2,2,20736]{3,2,1,0:T(2,128)(2,1)} %param.7) | copy-start | bytes 995332
  24.3 38.4 %all-to-all-start = ((bf16[256,2,576]{2,1,0:T(2,128)(2,1)}), bf16[256,2,576]{2,1,0:T(2,128)(2,1)S(1)}, u32[]{:S(2)}, u32[]{:S(2)}) async-start(bf16[256,2,576]{2,1,0:T(2,128)(2,1)} %shard_map.46), calls=%async_computation | async-start | bytes 1310720 | tf_op jit(solution)/shard_map/all_to_all | solution.py:224
  62.7 0.8 copy-start

commit v8 on v6

--- a/solution.py
+++ b/solution.py
@@ -30,8 +30,8 @@
     for t in range(count):
         wt_ref[t, F:WIDE, :] = jnp.zeros((WIDE - F, wt_ref.shape[2]), wt_ref.dtype)
         for c in range(count):
-            real = ext(m_ref[t, c, 0].astype(jnp.float32))
-            imag = ext(m_ref[t, c, 1].astype(jnp.float32))
+            real = ext(m_ref[0, t, c].astype(jnp.float32))
+            imag = ext(m_ref[1, t, c].astype(jnp.float32))
             top = real + pltpu.roll(-imag, P_SIZE, 1)
             bottom = imag + pltpu.roll(real, P_SIZE, 1)
             base = c * WIDE
@@ -153,7 +153,7 @@
     rows = 1024
     vmem = pl.BlockSpec(memory_space=pltpu.VMEM)
     w_scratch = [
-        pltpu.VMEM((m.shape[0], WIDE, m.shape[1] * WIDE), jnp.bfloat16) for m in m_list
+        pltpu.VMEM((m.shape[1], WIDE, m.shape[2] * WIDE), jnp.bfloat16) for m in m_list
     ]
     m_list = [jnp.pad(m, [(0, 0)] * 4 + [(0, LANE - P_SIZE)]) for m in m_list]
     return pl.pallas_call(
@@ -211,8 +211,8 @@
 def local(source, slope, quad, pair):
     place_x = lax.axis_index("gx")
     place_y = lax.axis_index("gy")
-    wq = lax.optimization_barrier(quad.astype(jnp.float32)).reshape(4, 4, 2, P_SIZE, P_SIZE)
-    wp = pair.reshape(2, 2, 2, P_SIZE, P_SIZE)
+    wq = quad.transpose(2, 0, 1, 3).reshape(2, 4, 4, P_SIZE, P_SIZE)
+    wp = pair.transpose(2, 0, 1, 3).reshape(2, 2, 2, P_SIZE, P_SIZE)
     group = jnp.arange(32, dtype=jnp.int32)
 
     f1 = factors(slope, place_x * 32 + group, place_y * 32 + group)

time: 118 us -> 113 us (0.958)
  other arithmetic: 4.59 us -> 2.36 us
  Pallas kernels: 29.1 us -> 27.7 us
  local copies, waits for them, and re-layouts: 17.5 us -> 16.2 us
    transpose x0 -> x2, local copies, waits for them, and re-layouts: none -> 3.19 us  [the longest x1 2.93 us: local(): wq = quad.transpose(2, 0, 1, 3).reshape(2, 4, 4, P_SIZE, P_SIZE)]
    pad x2, local copies, waits for them, and re-layouts: 5.88 us -> 2.72 us  [run_levels(): m_list = [jnp.pad(m, [(0, 0)] * 4 + [(0, LANE - P_SIZE)]) for m in m_list]]
    convert_element_type x1 -> x0, other arithmetic: 2.24 us -> none  [local(): quad.astype(jnp.float32)]
    pallas_call x2, Pallas kernels: 29.1 us -> 27.7 us  [run_levels(): pl.pallas_call(functools.partial(levels_kernel, levels, packed_in), out_s...]
    reshape x2, local copies, waits for them, and re-layouts: 7.46 us -> 6.14 us  [the longest x1 5.06 us: local(): wq = quad.transpose(2, 0, 1, 3).reshape(2, 4, 4, P_SIZE, P_SIZE)]
  transfers between devices with their start and end apart: 1 -> 1, of which waited for: 1 -> 1; matrix products, arithmetic and copies ran while one was open for 2% -> 3% of each run, Pallas kernels for 0% -> 0%
where the time goes in v8:
time: 113 us; the launch traced here: 112 us
  blocking collectives  30.7 us (27%)
  Pallas kernels  27.7 us (25%)
  waiting for transfers between devices  19.6 us (17%)
  local copies, waits for them, and re-layouts  16.2 us (14%)
  starting transfers between devices  15.7 us (14%)
  other arithmetic  2.36 us (2%)
    all_to_all x1, blocking collectives, local(): w = lax.all_to_all(y2, ('gx', 'gy'), 0, 0, tiled=True)  30.7 us
    pallas_call x2, Pallas kernels, run_levels(): pl.pallas_call(functools.partial(levels_kernel, levels, packed_in), out_s...  27.7 us
    all_to_all x1, waiting for transfers between devices, local(): z = lax.all_to_all(y1, ('gx', 'gy'), 0, 0, tiled=True)  19.6 us
    all_to_all x1, starting transfers between devices, local(): z = lax.all_to_all(y1, ('gx', 'gy'), 0, 0, tiled=True)  15.7 us
    reshape x1, local copies, waits for them, and re-layouts, local(): wq = quad.transpose(2, 0, 1, 3).reshape(2, 4, 4, P_SIZE, P_SIZE)  5.06 us
    transpose x1, local copies, waits for them, and re-layouts, local(): wq = quad.transpose(2, 0, 1, 3).reshape(2, 4, 4, P_SIZE, P_SIZE)  2.93 us
    pad x2, local copies, waits for them, and re-layouts, run_levels(): m_list = [jnp.pad(m, [(0, 0)] * 4 + [(0, LANE - P_SIZE)]) for m in m_list]  2.72 us
  transfers between devices with their start and end apart: 1, of which 1 were waited for; matrix products, arithmetic and copies ran while one was open for 3% of the time, Pallas kernels for 0%

profile of v8, /device:TPU:1, one launch (start us, length us, event | category | flops | bytes accessed | tf_op | source)
XLA Modules:
  0.0 112.4 jit_solution(522698652038703382)
XLA Ops:
  0.0 0.8 fusion.8
  0.8 2.9 %copy.11 = bf16[2,4,4,20736]{3,2,1,0:T(4,128)(2,1)} copy(bf16[2,4,4,20736]{3,0,2,1:T(2,128)(2,1)} %bitcast.25) | data formatting | bytes 2654208 | tf_op jit(solution)/shard_map/transpose | solution.py:214
  3.7 5.1 %reshape.61 = bf16[2,4,4,144,144]{4,3,2,1,0:T(8,128)(2,1)S(1)} reshape(bf16[2,4,4,20736]{3,2,1,0:T(4,128)(2,1)} %copy.11) | data formatting | bytes 2654208 | tf_op jit(solution)/shard_map/reshape | solution.py:214
  8.8 0.3 multiply_cosine_fusion.1
  9.1 0.1 fusion.6
  9.2 0.3 multiply_cosine_fusion
  9.5 0.1 fusion.4
  9.6 1.8 %pad.38.refs_0_ = bf16[2,4,4,144,256]{4,3,2,1,0:T(8,128)(2,1)} pad(bf16[2,4,4,144,144]{4,3,2,1,0:T(8,128)(2,1)S(1)} %reshape.61, bf16[]{:T(256)} %constant.37.clone.1), padding=0_0x0_0x0_0x0_0x0_112 | pad | bytes 3686402 | tf_op jit(solution)/shard_map/jit(_pad)/pad | solution.py:158
  11.4 0.7 pad_maximum_fusion.f_ref
  12.1 0.0 copy-start.1
  12.1 13.8 %shard_map.46 = bf16[256,2,576]{2,1,0:T(2,128)(2,1)} custom-call(bf16[288,1024]{1,0:T(8,128)(2,1)} %bitcast.26, f32[4,32,384]{2,1,0:T(8,128)} %pad_maximum_fusion.f_ref, bf16[2,4,4,144,256]{4,3,2,1,0:T(8,128)(2,1)} %pad.38.refs_0_), custom_call_target="tpu_custom_call" | custom-call | tf_op jit(solution)/shard_map/pallas_call | solution.py:159
  26.0 15.7 %all-to-all-start = ((bf16[256,2,576]{2,1,0:T(2,128)(2,1)}), bf16[256,2,576]{2,1,0:T(2,128)(2,1)S(1)}, u32[]{:S(2)}, u32[]{:S(2)}) async-start(bf16[256,2,576]{2,1,0:T(2,128)(2,1)} %shard_map.46), calls=%async_computation | async-start | bytes 1310720 | tf_op jit(solution)/shard_map/all_to_all | solution.py:222
  41.6 0.0 copy-done.1
  41.6 0.3 copy.12
  41.9 1.1 reshape.62
  43.0 0.9 pad.43.refs_1_
  43.9 0.1 fusion.2
  44.0 0.1 fusion
  44.1 0.7 pad_maximum_fusion.1.f_ref
  44.8 19.6 %all-to-all-done.x_ref = bf16[256,2,576]{2,1,0:T(2,128)(2,1)S(1)} async-done(((bf16[256,2,576]{2,1,0:T(2,128)(2,1)}), bf16[256,2,576]{2,1,0:T(2,128)(2,1)S(1)}, u32[]{:S(2)}, u32[]{:S(2)}) %all-to-all-start) | async-done | bytes 589856 | tf_op jit(solution)/shard_map/all_to_all | solution.py:222
  64.4 0.0 copy-start
  64.4 0.8 copy-done
  65.3 13.8 %shard_map.47 = bf16[256,2,576]{2,1,0:T(2,128)(2,1)} custom-call(bf16[256,2,576]{2,1,0:T(2,128)(2,1)} %copy-done, f32[4,32,384]{2,1,0:T(8,128)} %pad_maximum_fusion.1.f_ref, bf16[2,4,4,144,256]{4,3,2,1,0:T(8,128)(2,1)} %pad.38.refs_0_, bf16[2,2,2,144,256]{4,3,2,1,0:T(8,128)(2,1)} %pad.43.refs_1_), custom_call_target="tpu_custom_call" | custom-call | tf_op jit(solution)/shard_map/pallas_call | solution.py:159
  79.1 30.7 %all_to_all.10 = bf16[256,2,576]{2,1,0:T(2,128)(2,1)S(1)} all-to-all(bf16[256,2,576]{2,1,0:T(2,128)(2,1)} %shard_map.47), channel_id=1, replica_groups=mesh['gx'=8,'gy'=32] {'gx','gy'}, dimensions={0} | all-to-all | bytes 1179648 | tf_op jit(solution)/shard_map/all_to_all | solution.py:228
  109.8 1.0 copy.13
  110.8 0.3 copy.14
  111.2 1.2 %reshape.64 = bf16[288,1,1,1024]{3,0,2,1:T(8,128)(2,1)} reshape(bf16[2,144,4,256]{3,2,1,0:T(4,128)(2,1)S(1)} %copy.14) | data formatting | bytes 1179648 | tf_op jit(solution)/shard_map/reshape | solution.py:230
  (4 shorter events, 0.0 us)
Async XLA Ops:
  12.1 29.5 %copy-start.1 = (bf16[2,2,2,20736]{3,2,1,0:T(2,128)(2,1)S(1)}, bf16[2,2,2,20736]{3,2,1,0:T(2,128)(2,1)}, u32[]{:S(2)}) copy-start(bf16[2,2,2,20736]{3,2,1,0:T(2,128)(2,1)} %param.7) | copy-start | bytes 995332
  26.0 38.4 %all-to-all-start = ((bf16[256,2,576]{2,1,0:T(2,128)(2,1)}), bf16[256,2,576]{2,1,0:T(2,128)(2,1)S(1)}, u32[]{:S(2)}, u32[]{:S(2)}) async-start(bf16[256,2,576]{2,1,0:T(2,128)(2,1)} %shard_map.46), calls=%async_computation | async-start | bytes 1310720 | tf_op jit(solution)/shard_map/all_to_all | solution.py:222
  64.4 0.8 copy-start
